TPU v7x, 512 devices: a whole 4x4x16 slice. The times are simulated.
512 devices in a mesh: seq: 64 (over z, y), tp: 8 (over x, core).
Axes of the slice: x: 4, y: 4, z: 16, core: 2. Of those that a mesh axis runs over, the one named last changes fastest.
Arguments:
- cache: bfloat16 [2, 64, 512, 3072], P(None, 'seq', 'tp'), may hold values from -24 to 24
- cache_len: int32 [64], replicated, may hold values from 1 to 512, 16384 in all
- group: bfloat16 [3, 64, 256, 3072], P(None, 'seq', None, 'tp'), may hold values from -24 to 24
- group_req: int32 [64], replicated, may hold values from 0 to 63, each once
- req_order: int32 [64], replicated, may hold values from 0 to 63, each once
Outputs:
- context: bfloat16 [64, 256, 3072], P('seq', None, 'tp')
Inputs may be any that keep to these rules, and one draw needn't show every extreme that they name: `group_req`: each request once. `req_order`: each request once.
All inputs are finite; a program needn't handle non-finite values.
Results may differ from a plain program's by a relative error of at most 0.0042.
Values may be sent and summed in bfloat16 or wider, within the bound.
No kernel may reach another device: no remote copies, remote signals or barrier semaphores. Data moves between devices by JAX's collectives and lax.ppermute only.
A program may use at most 64 MiB of HBM per device.

v0:
```python
import math

import jax
import jax.numpy as jnp
from jax import lax
from jax.sharding import PartitionSpec as P

HD = 96


def inverse_table(permutation):
    numbers = jnp.arange(permutation.shape[0], dtype=jnp.int32)
    matches = permutation[None, :] == numbers[:, None]
    return jnp.sum(jnp.where(matches, numbers[None, :], 0), axis=1)


def online_part(queries, key_rows, value_rows, keep_rows, block_rows, block_count, factor):
    row_count = queries.shape[0]
    head_count = queries.shape[1]

    def add_block(block_index, carry):
        row_top, weight_sum, weighted = carry
        block_start = block_index * block_rows
        scores = (
            jnp.einsum("qhd,khd->hqk", queries, key_rows, preferred_element_type=jnp.float32)
            * factor
        )
        scores = jnp.where(keep_rows(block_start)[None], scores, -jnp.inf)
        new_top = jnp.maximum(row_top, jnp.max(scores, axis=-1))
        rescale = jnp.exp(row_top - new_top)
        weights = jnp.exp(scores - new_top[..., None]).astype(jnp.bfloat16)
        weight_sum = weight_sum * rescale + jnp.sum(weights, axis=-1, dtype=jnp.float32)
        weighted = weighted * rescale[..., None] + jnp.einsum(
            "hqk,khd->hqd", weights, value_rows, preferred_element_type=jnp.float32
        )
        return (new_top, weight_sum, weighted)

    start_top = jnp.full((head_count, row_count), -jnp.inf, jnp.float32)
    start_sum = jnp.zeros((head_count, row_count), jnp.float32)
    start_mixed = jnp.zeros((head_count, row_count, queries.shape[2]), jnp.float32)
    return lax.fori_loop(0, block_count, add_block, (start_top, start_sum, start_mixed))


def combine_parts(first_part, second_part):
    top_one, sum_one, mixed_one = first_part
    top_two, sum_two, mixed_two = second_part
    row_top = jnp.maximum(top_one, top_two)
    factor_one = jnp.exp(top_one - row_top)
    factor_two = jnp.exp(top_two - row_top)
    result = (factor_one[..., None] * mixed_one + factor_two[..., None] * mixed_two) / (
        factor_one * sum_one + factor_two * sum_two
    )[..., None]
    result = jnp.transpose(result, (1, 0, 2))
    return result.reshape(result.shape[0], -1).astype(jnp.bfloat16)


def shards(cache, cache_len, group, group_req, req_order):
    factor = 1.0 / math.sqrt(HD)
    slot_of = inverse_table(req_order)
    source_slot = jnp.take(slot_of, group_req)
    my_request = jnp.take(group_req, lax.axis_index("seq"))
    length = jnp.take(cache_len, my_request)
    row_count = group.shape[2]
    head_count = group.shape[3] // HD
    queries = group[0, 0].reshape(row_count, head_count, HD)
    new_keys = group[1, 0].reshape(row_count, head_count, HD)
    new_values = group[2, 0].reshape(row_count, head_count, HD)
    group_block = min(512, row_count)

    def causal_rows(block_start):
        key_index = block_start + jnp.arange(group_block, dtype=jnp.int32)
        return jnp.arange(row_count, dtype=jnp.int32)[:, None] >= key_index[None, :]

    group_part = online_part(
        queries, new_keys, new_values, causal_rows, group_block, row_count // group_block, factor
    )
    spread = lax.all_to_all(cache, "seq", split_axis=2, concat_axis=1, tiled=True)
    ordered = jnp.take(spread, source_slot, axis=1)
    moved = lax.all_to_all(
        lax.all_to_all(ordered, "seq", split_axis=1, concat_axis=2, tiled=True),
        "tp",
        split_axis=3,
        concat_axis=2,
        tiled=True,
    )
    position_count = moved.shape[2]
    old_keys = moved[0, 0].reshape(position_count, head_count, HD)
    old_values = moved[1, 0].reshape(position_count, head_count, HD)
    cache_block = min(512, position_count)

    def live_rows(block_start):
        positions = block_start + jnp.arange(cache_block, dtype=jnp.int32)
        return (positions < length)[None, :]

    block_total = position_count // cache_block
    cache_part = online_part(
        queries, old_keys, old_values, live_rows, cache_block, block_total, factor
    )
    context = combine_parts(cache_part, group_part)
    return context[None]


def solution(mesh):
    in_specs = (P(None, "seq", "tp", None), P(), P(None, "seq", None, "tp"), P(), P())
    out_specs = P("seq", None, "tp")
    return jax.shard_map(shards, mesh=mesh, in_specs=in_specs, out_specs=out_specs, check_vma=False)
```

profile of v0, /device:TPU:1, one launch (start us, length us, event | category | flops | bytes accessed | tf_op | source)
XLA Modules:
  0.0 145.0 jit_solution(2119875691103192818)
XLA Ops:
  0.0 2.9 %copy.47 = bf16[2,1,64,3072]{3,0,1,2:T(2,128)(2,1)} copy(bf16[2,1,64,3072]{3,2,1,0:T(8,128)(2,1)} %param.5) | data formatting | bytes 1572864 | tf_op args[0]
  2.9 19.3 %all-to-all-start = ((bf16[2,1,64,3072]{3,0,1,2:T(2,128)(2,1)}), bf16[2,1,64,3072]{3,0,1,2:T(2,128)(2,1)S(1)}, u32[]{:S(2)}, u32[]{:S(2)}) async-start(bf16[2,1,64,3072]{3,0,1,2:T(2,128)(2,1)} %copy.47), calls=%async_computation | async-start | bytes 1572864 | tf_op jit(solution)/shard_map/all_to_all | solution.py:77
  22.2 0.1 select_reduce_fusion
  22.3 0.8 gather_fusion
  23.1 39.8 %all-to-all-done = bf16[2,1,64,3072]{3,0,1,2:T(2,128)(2,1)S(1)} async-done(((bf16[2,1,64,3072]{3,0,1,2:T(2,128)(2,1)}), bf16[2,1,64,3072]{3,0,1,2:T(2,128)(2,1)S(1)}, u32[]{:S(2)}, u32[]{:S(2)}) %all-to-all-start) | async-done | bytes 786464 | tf_op jit(solution)/shard_map/all_to_all | solution.py:77
  63.0 2.1 %gather_fusion.1 = bf16[64,2,3072]{2,1,0:T(2,128)(2,1)S(1)} fusion(bf16[2,64,3072]{2,0,1:T(2,128)(2,1)S(1)} %bitcast.96, s32[1024]{0:T(1024)S(1)} %pad_clamp_fusion), kind=kCustom, calls=%fused_computation.1 | custom fusion | bytes 1573120 | tf_op jit(solution)/shard_map/jit(_take)/gather | solution.py:78
  65.1 0.8 fusion.10
  65.9 48.8 %all_to_all.39 = bf16[2,64,1,3072]{3,0,2,1:T(2,128)(2,1)S(1)} all-to-all(bf16[2,64,1,3072]{3,0,2,1:T(2,128)(2,1)S(1)} %fusion.10), channel_id=1, replica_groups=mesh['seq'=64,'tp'=8] {'seq'}, dimensions={1} | all-to-all | bytes 1572864 | tf_op jit(solution)/shard_map/all_to_all | solution.py:80
  114.7 1.3 copy.49
  116.0 0.0 copy-start.3
  116.1 1.9 %reshape.180 = bf16[8,2,24576]{2,1,0:T(2,128)(2,1)} reshape(bf16[3072,1,2,64]{3,2,1,0:T(2,128)(2,1)S(1)} %bitcast.94) | data formatting | bytes 1572864
  118.0 8.8 %all-to-all-start.2 = ((bf16[8,2,24576]{2,1,0:T(2,128)(2,1)}), bf16[8,2,24576]{2,1,0:T(2,128)(2,1)S(1)}, u32[]{:S(2)}, u32[]{:S(2)}) async-start(bf16[8,2,24576]{2,1,0:T(2,128)(2,1)} %reshape.180), calls=%async_computation.2 | async-start | bytes 1572864 | tf_op jit(solution)/shard_map/all_to_all | solution.py:79
  126.8 0.1 fusion.27
  126.9 0.7 dynamic-slice.4
  128.2 0.7 dynamic-slice.5
  128.8 0.1 copy.51
  129.0 0.1 copy.53
  129.2 0.8 copy.56
  130.7 0.4 fusion.28
  131.1 0.2 convert_reduce_fusion.1
  131.3 7.7 %all-to-all-done.2 = bf16[8,2,24576]{2,1,0:T(2,128)(2,1)S(1)} async-done(((bf16[8,2,24576]{2,1,0:T(2,128)(2,1)}), bf16[8,2,24576]{2,1,0:T(2,128)(2,1)S(1)}, u32[]{:S(2)}, u32[]{:S(2)}) %all-to-all-start.2) | async-done | bytes 786464 | tf_op jit(solution)/shard_map/all_to_all | solution.py:79
  139.0 1.0 reshape.181
  140.0 1.2 copy.50
  141.2 0.1 fusion.26
  141.3 0.4 reshape_squeeze.15
  141.6 0.4 reshape_squeeze.18
  142.0 0.1 copy-done.2
  142.1 0.4 bitcast_reduce_fusion
  142.5 0.5 convert_reduce_fusion
  143.1 0.3 fusion.7
  143.4 0.7 fusion.9
  144.2 0.8 copy.58
  (19 shorter events, 0.1 us)
Async XLA Ops:
  0.0 22.1 %copy-start.4 = (s32[64]{0:T(128)S(1)}, s32[64]{0:T(128)}, u32[]{:S(2)}) copy-start(s32[64]{0:T(128)} %param.8) | copy-start | bytes 772
  0.0 22.2 %copy-start.5 = (s32[64]{0:T(128)S(1)}, s32[64]{0:T(128)}, u32[]{:S(2)}) copy-start(s32[64]{0:T(128)} %param.9) | copy-start | bytes 772
  2.9 60.1 %all-to-all-start = ((bf16[2,1,64,3072]{3,0,1,2:T(2,128)(2,1)}), bf16[2,1,64,3072]{3,0,1,2:T(2,128)(2,1)S(1)}, u32[]{:S(2)}, u32[]{:S(2)}) async-start(bf16[2,1,64,3072]{3,0,1,2:T(2,128)(2,1)} %copy.47), calls=%async_computation | async-start | bytes 1572864 | tf_op jit(solution)/shard_map/all_to_all | solution.py:77
  116.0 10.8 %copy-start.3 = (bf16[3,1,256,384]{3,2,1,0:T(8,128)(2,1)S(1)}, bf16[3,1,256,384]{3,2,1,0:T(8,128)(2,1)}, u32[]{:S(2)}) copy-start(bf16[3,1,256,384]{3,2,1,0:T(8,128)(2,1)} %param.7) | copy-start | bytes 1769476
  116.0 12.1 %copy-start.6 = (s32[64]{0:T(128)S(1)}, s32[64]{0:T(128)}, u32[]{:S(2)}) copy-start(s32[64]{0:T(128)} %param.6) | copy-start | bytes 772
  118.0 21.0 %all-to-all-start.2 = ((bf16[8,2,24576]{2,1,0:T(2,128)(2,1)}), bf16[8,2,24576]{2,1,0:T(2,128)(2,1)S(1)}, u32[]{:S(2)}, u32[]{:S(2)}) async-start(bf16[8,2,24576]{2,1,0:T(2,128)(2,1)} %reshape.180), calls=%async_computation.2 | async-start | bytes 1572864 | tf_op jit(solution)/shard_map/all_to_all | solution.py:79
  129.0 2.3 %copy-start.1 = (bf16[1,1,256,384]{2,3,1,0:T(8,128)(2,1)}, bf16[1,1,256,384]{2,3,1,0:T(8,128)(2,1)S(1)}, u32[]{:S(2)}) copy-start(bf16[1,1,256,384]{2,3,1,0:T(8,128)(2,1)S(1)} %copy.51) | copy-start | bytes 589828
  141.2 0.9 copy-start.2
  142.1 1.0 copy-start
where the time goes:
time: 145 us
  blocking collectives  48.8 us (34%)
  waiting for transfers between devices  47.5 us (33%)
  starting transfers between devices  28.1 us (19%)
  local copies, waits for them, and re-layouts  15.4 us (11%)
  matrix products  1.87 us (1%)
  other arithmetic  1.62 us (1%)
  between operations  1.57 us (1%)
    all_to_all x1, blocking collectives, shards(): lax.all_to_all(ordered, 'seq', split_axis=1, concat_axis=2, tiled=True)  48.8 us
    all_to_all x1, waiting for transfers between devices, shards(): lax.all_to_all(cache, 'seq', split_axis=2, concat_axis=1, tiled=True)  39.8 us
    all_to_all x1, starting transfers between devices, shards(): lax.all_to_all(cache, 'seq', split_axis=2, concat_axis=1, tiled=True)  19.3 us
    all_to_all x1, starting transfers between devices, shards(): lax.all_to_all(lax.all_to_all(ordered, 'seq', split_axis=1, concat_axis=2...  8.85 us
    all_to_all x1, waiting for transfers between devices, shards(): lax.all_to_all(lax.all_to_all(ordered, 'seq', split_axis=1, concat_axis=2...  7.7 us
    unnamed x17, local copies, waits for them, and re-layouts  5.91 us
  transfers between devices with their start and end apart: 2, of which 2 were waited for; matrix products, arithmetic and copies ran while one was open for 3% of the time, Pallas kernels for 0%

commit v1 on v0

v1 whole, which is shorter than its diff:
```python
import math

import jax
import jax.numpy as jnp
from jax import lax
from jax.sharding import PartitionSpec as P

HD = 96


def inverse_table(permutation):
    numbers = jnp.arange(permutation.shape[0], dtype=jnp.int32)
    matches = permutation[None, :] == numbers[:, None]
    return jnp.sum(jnp.where(matches, numbers[None, :], 0), axis=1)


def partial_part(queries, key_rows, value_rows, keep, factor):
    scores = (
        jnp.einsum("qhd,khd->hqk", queries, key_rows, preferred_element_type=jnp.float32)
        * factor
    )
    scores = jnp.where(keep[None], scores, -jnp.inf)
    row_top = jnp.max(scores, axis=-1)
    weights = jnp.exp(scores - row_top[..., None]).astype(jnp.bfloat16)
    weight_sum = jnp.sum(weights, axis=-1, dtype=jnp.float32)
    weighted = jnp.einsum(
        "hqk,khd->hqd", weights, value_rows, preferred_element_type=jnp.float32
    )
    return (row_top, weight_sum, weighted)


def combine_parts(first_part, second_part):
    top_one, sum_one, mixed_one = first_part
    top_two, sum_two, mixed_two = second_part
    row_top = jnp.maximum(top_one, top_two)
    factor_one = jnp.exp(top_one - row_top)
    factor_two = jnp.exp(top_two - row_top)
    result = (factor_one[..., None] * mixed_one + factor_two[..., None] * mixed_two) / (
        factor_one * sum_one + factor_two * sum_two
    )[..., None]
    result = jnp.transpose(result, (1, 0, 2))
    return result.reshape(result.shape[0], -1).astype(jnp.bfloat16)


def permute_rows(rows, order):
    count = order.shape[0]
    pieces = rows.reshape(count, rows.shape[0] // count, rows.shape[1])
    spread = lax.all_to_all(pieces, "seq", split_axis=0, concat_axis=0, tiled=True)
    ordered = jnp.take(spread, order, axis=0)
    gathered = lax.all_to_all(ordered, "seq", split_axis=0, concat_axis=0, tiled=True)
    return gathered.reshape(rows.shape)


def shards(cache, cache_len, group, group_req, req_order):
    factor = 1.0 / math.sqrt(HD)
    slot_of = inverse_table(req_order)
    index_of = inverse_table(group_req)
    query_source = jnp.take(index_of, req_order)
    cache_source = jnp.take(slot_of, group_req)
    me = lax.axis_index("seq")
    slot_request = jnp.take(req_order, me)
    slot_length = jnp.take(cache_len, slot_request)

    row_count = group.shape[2]
    feature_count = group.shape[3]
    head_count = feature_count // HD
    queries = group[0, 0]
    new_keys = group[1, 0].reshape(row_count, head_count, HD)
    new_values = group[2, 0].reshape(row_count, head_count, HD)

    local = lax.all_to_all(cache[:, 0], "tp", split_axis=2, concat_axis=1, tiled=True)
    position_count = local.shape[1]
    old_keys = local[0].reshape(position_count, head_count, HD)
    old_values = local[1].reshape(position_count, head_count, HD)

    slot_queries = permute_rows(queries, query_source).reshape(row_count, head_count, HD)
    live = (jnp.arange(position_count, dtype=jnp.int32) < slot_length)[None, :]
    top_c, sum_c, mixed_c = partial_part(slot_queries, old_keys, old_values, live, factor)
    packed = jnp.concatenate(
        [
            jnp.transpose(mixed_c, (1, 0, 2)).reshape(row_count, feature_count),
            jnp.transpose(top_c),
            jnp.transpose(sum_c),
        ],
        axis=1,
    )
    back = permute_rows(packed, cache_source)
    cache_part = (
        jnp.transpose(back[:, feature_count : feature_count + head_count]),
        jnp.transpose(back[:, feature_count + head_count :]),
        jnp.transpose(back[:, :feature_count].reshape(row_count, head_count, HD), (1, 0, 2)),
    )

    causal = jnp.arange(row_count, dtype=jnp.int32)[:, None] >= jnp.arange(
        row_count, dtype=jnp.int32
    )[None, :]
    group_part = partial_part(
        queries.reshape(row_count, head_count, HD), new_keys, new_values, causal, factor
    )
    context = combine_parts(cache_part, group_part)
    return context[None]


def solution(mesh):
    in_specs = (P(None, "seq", "tp", None), P(), P(None, "seq", None, "tp"), P(), P())
    out_specs = P("seq", None, "tp")
    return jax.shard_map(shards, mesh=mesh, in_specs=in_specs, out_specs=out_specs, check_vma=False)
```

time: 145 us -> 168 us (1.16); the launches traced: 145 us -> 165 us
  blocking collectives: 48.8 us -> 0 us
  waiting for transfers between devices: 47.5 us -> 89.1 us
  starting transfers between devices: 28.1 us -> 48 us
  local copies, waits for them, and re-layouts: 15.4 us -> 20.1 us
  other arithmetic: 1.62 us -> 3.87 us
    all_to_all x1 -> x0, blocking collectives: 48.8 us -> none  [shards(): lax.all_to_all(ordered, 'seq', split_axis=1, concat_axis=2, tiled=True)]
    all_to_all x2 -> x5, waiting for transfers between devices: 47.5 us -> 89.1 us  [the longest x2 40.2 us: permute_rows(): lax.all_to_all(pieces, 'seq', split_axis=0, concat_axis=0, tiled=True)]
    all_to_all x2 -> x5, starting transfers between devices: 28.1 us -> 48 us  [the longest x2 25.6 us: permute_rows(): lax.all_to_all(pieces, 'seq', split_axis=0, concat_axis=0, tiled=True)]
    another operation x4 -> x6, local copies, waits for them, and re-layouts: 2.04 us -> 3.93 us  [the longest x1 1.14 us: shards(): permute_rows(queries, query_source).reshape(row_count, head_count, HD)]
    slice x2, local copies, waits for them, and re-layouts: 0.21 us -> 2.07 us  [shards(): new_keys = group[1, 0].reshape(row_count, head_count, HD)]
    gather x2 -> x4, local copies, waits for them, and re-layouts: 2.92 us -> 4.14 us  [the longest x2 2.57 us: permute_rows(): ordered = jnp.take(spread, order, axis=0)]
    unnamed x17 -> x16, local copies, waits for them, and re-layouts: 5.91 us -> 6.19 us
  transfers between devices with their start and end apart: 2 -> 5, of which waited for: 2 -> 5; matrix products, arithmetic and copies ran while one was open for 3% -> 9% of each run, Pallas kernels for 0% -> 0%
where the time goes in v1:
time: 168 us; the launch traced here: 165 us
  waiting for transfers between devices  89.1 us (53%)
  starting transfers between devices  48 us (29%)
  local copies, waits for them, and re-layouts  20.1 us (12%)
  other arithmetic  3.87 us (2%)
  matrix products  1.94 us (1%)
  between operations  1.72 us (1%)
    all_to_all x2, waiting for transfers between devices, permute_rows(): lax.all_to_all(pieces, 'seq', split_axis=0, concat_axis=0, tiled=True)  40.2 us
    all_to_all x2, waiting for transfers between devices, permute_rows(): lax.all_to_all(ordered, 'seq', split_axis=0, concat_axis=0, tiled=True)  40.2 us
    all_to_all x2, starting transfers between devices, permute_rows(): lax.all_to_all(pieces, 'seq', split_axis=0, concat_axis=0, tiled=True)  25.6 us
    all_to_all x2, starting transfers between devices, permute_rows(): lax.all_to_all(ordered, 'seq', split_axis=0, concat_axis=0, tiled=True)  14.2 us
    all_to_all x1, waiting for transfers between devices, shards(): lax.all_to_all(cache[:, 0], 'tp', split_axis=2, concat_axis=1, tiled=True)  8.66 us
    all_to_all x1, starting transfers between devices, shards(): lax.all_to_all(cache[:, 0], 'tp', split_axis=2, concat_axis=1, tiled=True)  8.14 us
    unnamed x16, local copies, waits for them, and re-layouts  6.19 us
  transfers between devices with their start and end apart: 5, of which 5 were waited for; matrix products, arithmetic and copies ran while one was open for 9% of the time, Pallas kernels for 0%

profile of v1, /device:TPU:1, one launch (start us, length us, event | category | flops | bytes accessed | tf_op | source)
XLA Modules:
  0.0 164.7 jit_solution(6261947117886503793)
XLA Ops:
  0.0 1.9 %fusion.18 = (bf16[1,1,256,384]{3,2,1,0:T(8,128)(2,1)}, bf16[1,1,256,384]{3,2,1,0:T(8,128)(2,1)S(1)}, bf16[1,1,256,384]{3,2,1,0:T(8,128)(2,1)S(1)}) fusion(bf16[3,1,256,384]{3,2,1,0:T(8,128)(2,1)} %param.9), kind=kLoop, calls=%fused_computation.52 | loop fusion | bytes 1179648 | tf_op jit(solution)/shard_map/slice | solution.py:68
  1.9 0.7 reshape_squeeze.18
  2.7 19.5 %all-to-all-start = ((bf16[64,4,384]{2,1,0:T(4,128)(2,1)}), bf16[64,4,384]{2,1,0:T(4,128)(2,1)}, u32[]{:S(2)}, u32[]{:S(2)}) async-start(bf16[64,4,384]{2,1,0:T(4,128)(2,1)} %reshape_squeeze.18), calls=%async_computation | async-start | bytes 393216 | tf_op jit(solution)/shard_map/all_to_all | solution.py:48
  22.2 1.9 %copy.45 = bf16[2,1,64,3072]{2,0,3,1:T(2,128)(2,1)S(1)} copy(bf16[2,1,64,3072]{3,2,1,0:T(8,128)(2,1)S(1)} %copy-done.1) | data formatting | bytes 1572864 | tf_op args[0]
  24.1 1.1 bitcast_bitcast_fusion
  25.3 1.9 %reshape.168 = bf16[8,2,24576]{2,1,0:T(2,128)(2,1)} reshape(bf16[3072,2,64]{2,1,0:T(2,128)(2,1)S(1)} %bitcast_bitcast_fusion) | data formatting | bytes 1572864
  27.2 12.2 %all-to-all-done = bf16[64,4,384]{2,1,0:T(4,128)(2,1)} async-done(((bf16[64,4,384]{2,1,0:T(4,128)(2,1)}), bf16[64,4,384]{2,1,0:T(4,128)(2,1)}, u32[]{:S(2)}, u32[]{:S(2)}) %all-to-all-start) | async-done | bytes 196640 | tf_op jit(solution)/shard_map/all_to_all | solution.py:48
  39.4 8.1 %all-to-all-start.2 = ((bf16[8,2,24576]{2,1,0:T(2,128)(2,1)}), bf16[8,2,24576]{2,1,0:T(2,128)(2,1)S(1)}, u32[]{:S(2)}, u32[]{:S(2)}) async-start(bf16[8,2,24576]{2,1,0:T(2,128)(2,1)} %reshape.168), calls=%async_computation.2 | async-start | bytes 1572864 | tf_op jit(solution)/shard_map/all_to_all | solution.py:71
  47.6 0.8 gather_fusion.3
  48.4 1.7 %gather_fusion = bf16[64,4,384]{2,1,0:T(4,128)(2,1)S(1)} fusion(bf16[64,4,384]{2,1,0:T(4,128)(2,1)} %all-to-all-done, s32[1024]{0:T(1024)S(1)} %pad_clamp_fusion.1), kind=kCustom, calls=%fused_computation.2 | custom fusion | bytes 393472 | tf_op jit(solution)/shard_map/jit(_take)/gather | solution.py:49
  50.1 0.9 broadcast_select_fusion.1
  51.0 8.7 %all-to-all-done.2 = bf16[8,2,24576]{2,1,0:T(2,128)(2,1)S(1)} async-done(((bf16[8,2,24576]{2,1,0:T(2,128)(2,1)}), bf16[8,2,24576]{2,1,0:T(2,128)(2,1)S(1)}, u32[]{:S(2)}, u32[]{:S(2)}) %all-to-all-start.2) | async-done | bytes 786464 | tf_op jit(solution)/shard_map/all_to_all | solution.py:71
  59.7 5.4 %all-to-all-start.1 = ((bf16[64,4,384]{2,1,0:T(4,128)(2,1)}), bf16[64,4,384]{2,1,0:T(4,128)(2,1)}, u32[]{:S(2)}, u32[]{:S(2)}) async-start(bf16[64,4,384]{2,1,0:T(4,128)(2,1)} %broadcast_select_fusion.1), calls=%async_computation.1 | async-start | bytes 393216 | tf_op jit(solution)/shard_map/all_to_all | solution.py:50
  65.1 0.7 dynamic-slice.4
  66.5 0.7 dynamic-slice.5
  67.9 1.0 reshape.169
  68.9 1.2 copy.46
  70.9 11.9 %all-to-all-done.1 = bf16[64,4,384]{2,1,0:T(4,128)(2,1)} async-done(((bf16[64,4,384]{2,1,0:T(4,128)(2,1)}), bf16[64,4,384]{2,1,0:T(4,128)(2,1)}, u32[]{:S(2)}, u32[]{:S(2)}) %all-to-all-start.1) | async-done | bytes 196640 | tf_op jit(solution)/shard_map/all_to_all | solution.py:50
  82.8 1.1 reshape_reshape.3
  83.9 0.5 fusion
  84.5 0.6 convert_reduce_fusion
  85.1 0.7 convolution_bitcast_fusion.1
  86.1 0.4 concatenate.10
  86.8 1.0 pad_maximum_fusion
  87.7 6.1 %all-to-all-start.3 = ((f32[64,4,392]{2,1,0:T(4,128)}), f32[64,4,392]{2,1,0:T(4,128)S(1)}, u32[]{:S(2)}, u32[]{:S(2)}) async-start(f32[64,4,392]{2,1,0:T(4,128)} %pad_maximum_fusion), calls=%async_computation.3 | async-start | bytes 1048576 | tf_op jit(solution)/shard_map/all_to_all | solution.py:48
  94.0 0.8 gather_fusion.2
  94.8 28.1 %all-to-all-done.3 = f32[64,4,392]{2,1,0:T(4,128)S(1)} async-done(((f32[64,4,392]{2,1,0:T(4,128)}), f32[64,4,392]{2,1,0:T(4,128)S(1)}, u32[]{:S(2)}, u32[]{:S(2)}) %all-to-all-start.3) | async-done | bytes 401440 | tf_op jit(solution)/shard_map/all_to_all | solution.py:48
  122.9 0.9 gather_fusion.1
  123.8 1.0 broadcast_select_fusion
  124.8 8.8 %all-to-all-start.4 = ((f32[64,4,392]{2,1,0:T(4,128)}), f32[64,4,392]{2,1,0:T(4,128)S(1)}, u32[]{:S(2)}, u32[]{:S(2)}) async-start(f32[64,4,392]{2,1,0:T(4,128)} %broadcast_select_fusion), calls=%async_computation.4 | async-start | bytes 1048576 | tf_op jit(solution)/shard_map/all_to_all | solution.py:50
  134.6 28.3 %all-to-all-done.4 = f32[64,4,392]{2,1,0:T(4,128)S(1)} async-done(((f32[64,4,392]{2,1,0:T(4,128)}), f32[64,4,392]{2,1,0:T(4,128)S(1)}, u32[]{:S(2)}, u32[]{:S(2)}) %all-to-all-start.4) | async-done | bytes 401440 | tf_op jit(solution)/shard_map/all_to_all | solution.py:50
  163.9 0.8 copy.60
  (41 shorter events, 3.6 us)
Async XLA Ops:
  0.0 22.2 %copy-start.1 = (bf16[2,1,64,3072]{3,2,1,0:T(8,128)(2,1)S(1)}, bf16[2,1,64,3072]{3,2,1,0:T(8,128)(2,1)}, u32[]{:S(2)}) copy-start(bf16[2,1,64,3072]{3,2,1,0:T(8,128)(2,1)} %param.7) | copy-start | bytes 2359300
  2.7 36.7 %all-to-all-start = ((bf16[64,4,384]{2,1,0:T(4,128)(2,1)}), bf16[64,4,384]{2,1,0:T(4,128)(2,1)}, u32[]{:S(2)}, u32[]{:S(2)}) async-start(bf16[64,4,384]{2,1,0:T(4,128)(2,1)} %reshape_squeeze.18), calls=%async_computation | async-start | bytes 393216 | tf_op jit(solution)/shard_map/all_to_all | solution.py:48
  24.1 3.1 %copy-start.2 = (s32[64]{0:T(128)S(1)}, s32[64]{0:T(128)}, u32[]{:S(2)}) copy-start(s32[64]{0:T(128)} %param.11) | copy-start | bytes 772
  25.3 22.3 %copy-start.3 = (s32[64]{0:T(128)S(1)}, s32[64]{0:T(128)}, u32[]{:S(2)}) copy-start(s32[64]{0:T(128)} %param.10) | copy-start | bytes 772
  27.2 39.3 %copy-start.4 = (s32[64]{0:T(128)S(1)}, s32[64]{0:T(128)}, u32[]{:S(2)}) copy-start(s32[64]{0:T(128)} %param.8) | copy-start | bytes 772
  39.4 20.3 %all-to-all-start.2 = ((bf16[8,2,24576]{2,1,0:T(2,128)(2,1)}), bf16[8,2,24576]{2,1,0:T(2,128)(2,1)S(1)}, u32[]{:S(2)}, u32[]{:S(2)}) async-start(bf16[8,2,24576]{2,1,0:T(2,128)(2,1)} %reshape.168), calls=%async_computation.2 | async-start | bytes 1572864 | tf_op jit(solution)/shard_map/all_to_all | solution.py:71
  59.7 23.1 %all-to-all-start.1 = ((bf16[64,4,384]{2,1,0:T(4,128)(2,1)}), bf16[64,4,384]{2,1,0:T(4,128)(2,1)}, u32[]{:S(2)}, u32[]{:S(2)}) async-start(bf16[64,4,384]{2,1,0:T(4,128)(2,1)} %broadcast_select_fusion.1), calls=%async_computation.1 | async-start | bytes 393216 | tf_op jit(solution)/shard_map/all_to_all | solution.py:50
  87.7 35.2 %all-to-all-start.3 = ((f32[64,4,392]{2,1,0:T(4,128)}), f32[64,4,392]{2,1,0:T(4,128)S(1)}, u32[]{:S(2)}, u32[]{:S(2)}) async-start(f32[64,4,392]{2,1,0:T(4,128)} %pad_maximum_fusion), calls=%async_computation.3 | async-start | bytes 1048576 | tf_op jit(solution)/shard_map/all_to_all | solution.py:48
  93.9 39.8 %copy-start = (bf16[1,1,256,384]{3,2,1,0:T(8,128)(2,1)S(1)}, bf16[1,1,256,384]{3,2,1,0:T(8,128)(2,1)}, u32[]{:S(2)}) copy-start(bf16[1,1,256,384]{3,2,1,0:T(8,128)(2,1)} %get-tuple-element.37) | copy-start | bytes 589828
  124.8 38.1 %all-to-all-start.4 = ((f32[64,4,392]{2,1,0:T(4,128)}), f32[64,4,392]{2,1,0:T(4,128)S(1)}, u32[]{:S(2)}, u32[]{:S(2)}) async-start(f32[64,4,392]{2,1,0:T(4,128)} %broadcast_select_fusion), calls=%async_computation.4 | async-start | bytes 1048576 | tf_op jit(solution)/shard_map/all_to_all | solution.py:50

commit v2 on v1

v2 whole, which is shorter than its diff:
```python
import math

import jax
import jax.numpy as jnp
from jax import lax
from jax.sharding import PartitionSpec as P

HD = 96


def inverse_table(permutation):
    numbers = jnp.arange(permutation.shape[0], dtype=jnp.int32)
    matches = permutation[None, :] == numbers[:, None]
    return jnp.sum(jnp.where(matches, numbers[None, :], 0), axis=1)


def partial_part(queries, key_rows, value_rows, keep, factor):
    scores = (
        jnp.einsum("qhd,khd->hqk", queries, key_rows, preferred_element_type=jnp.float32)
        * factor
    )
    scores = jnp.where(keep[None], scores, -jnp.inf)
    row_top = jnp.max(scores, axis=-1)
    weights = jnp.exp(scores - row_top[..., None]).astype(jnp.bfloat16)
    weight_sum = jnp.sum(weights, axis=-1, dtype=jnp.float32)
    weighted = jnp.einsum(
        "hqk,khd->hqd", weights, value_rows, preferred_element_type=jnp.float32
    )
    return (row_top, weight_sum, weighted)


def combine_parts(first_part, second_part):
    top_one, sum_one, mixed_one = first_part
    top_two, sum_two, mixed_two = second_part
    row_top = jnp.maximum(top_one, top_two)
    factor_one = jnp.exp(top_one - row_top)
    factor_two = jnp.exp(top_two - row_top)
    result = (factor_one[..., None] * mixed_one + factor_two[..., None] * mixed_two) / (
        factor_one * sum_one + factor_two * sum_two
    )[..., None]
    result = jnp.transpose(result, (1, 0, 2))
    return result.reshape(result.shape[0], -1).astype(jnp.bfloat16)


def shards(cache, cache_len, group, group_req, req_order):
    factor = 1.0 / math.sqrt(HD)
    slot_of = inverse_table(req_order)
    source_slot = jnp.take(slot_of, group_req)
    my_request = jnp.take(group_req, lax.axis_index("seq"))
    length = jnp.take(cache_len, my_request)
    row_count = group.shape[2]
    feature_count = group.shape[3]
    head_count = feature_count // HD
    queries = group[0, 0].reshape(row_count, head_count, HD)
    new_keys = group[1, 0].reshape(row_count, head_count, HD)
    new_values = group[2, 0].reshape(row_count, head_count, HD)

    causal = jnp.arange(row_count, dtype=jnp.int32)[:, None] >= jnp.arange(
        row_count, dtype=jnp.int32
    )[None, :]
    group_part = partial_part(queries, new_keys, new_values, causal, factor)

    seq_count = source_slot.shape[0]
    tp_count = cache.shape[3] // feature_count
    local_positions = cache.shape[2]
    by_position = jnp.transpose(cache[:, 0], (1, 0, 2))
    spread = lax.all_to_all(by_position, "seq", split_axis=0, concat_axis=0, tiled=True)
    ordered = jnp.take(spread, source_slot, axis=0)
    ordered = ordered.reshape(seq_count, 2, tp_count, feature_count)
    ordered = jnp.transpose(ordered, (0, 2, 1, 3))
    moved = lax.all_to_all(
        ordered.reshape(seq_count * tp_count, 2, feature_count),
        ("seq", "tp"),
        split_axis=0,
        concat_axis=0,
        tiled=True,
    )
    row_total = moved.shape[0]
    old_keys = moved[:, 0].reshape(row_total, head_count, HD)
    old_values = moved[:, 1].reshape(row_total, head_count, HD)
    rows = jnp.arange(row_total, dtype=jnp.int32)
    positions = (rows % tp_count) * local_positions + rows // tp_count
    live = (positions < length)[None, :]
    cache_part = partial_part(queries, old_keys, old_values, live, factor)
    context = combine_parts(cache_part, group_part)
    return context[None]


def solution(mesh):
    in_specs = (P(None, "seq", "tp", None), P(), P(None, "seq", None, "tp"), P(), P())
    out_specs = P("seq", None, "tp")
    return jax.shard_map(shards, mesh=mesh, in_specs=in_specs, out_specs=out_specs, check_vma=False)
```

time: 168 us -> 134 us (0.80); the launches traced: 165 us -> 134 us
  starting transfers between devices: 48 us -> 33.4 us
  waiting for transfers between devices: 89.1 us -> 82.5 us
  local copies, waits for them, and re-layouts: 20.1 us -> 14.3 us
  other arithmetic: 3.87 us -> 1.06 us
    all_to_all x5 -> x2, starting transfers between devices: 48 us -> 33.4 us  [the longest x1 19.3 us: shards(): lax.all_to_all(by_position, 'seq', split_axis=0, concat_axis=0, tiled=True)]
    all_to_all x5 -> x2, waiting for transfers between devices: 89.1 us -> 82.5 us  [the longest x1 42.6 us: shards(): lax.all_to_all(ordered.reshape(seq_count * tp_count, 2, feature_count), (...]
    unnamed x16 -> x15, local copies, waits for them, and re-layouts: 6.19 us -> 2.94 us
    another operation x6 -> x2, local copies, waits for them, and re-layouts: 3.93 us -> 1.2 us  [the longest x1 0.61 us: shards(): my_request = jnp.take(group_req, lax.axis_index('seq'))]
    slice x5 -> x4, local copies, waits for them, and re-layouts: 0.53 us -> 3.23 us  [the longest x2 2.09 us: shards(): old_keys = moved[:, 0].reshape(row_total, head_count, HD)]
    slice x2 -> x1, local copies, waits for them, and re-layouts: 2.07 us -> 0.15 us  [shards(): new_keys = group[1, 0].reshape(row_count, head_count, HD)]
    select_n x4 -> x1, other arithmetic: 1.83 us -> 0.01 us  [shards(): source_slot = jnp.take(slot_of, group_req)]
    gather x4 -> x3, local copies, waits for them, and re-layouts: 4.14 us -> 3.42 us  [the longest x2 2.63 us: shards(): ordered = jnp.take(spread, source_slot, axis=0)]
  transfers between devices with their start and end apart: 5 -> 2, of which waited for: 5 -> 2; matrix products, arithmetic and copies ran while one was open for 9% -> 3% of each run, Pallas kernels for 0% -> 0%
where the time goes in v2:
time: 134 us
  waiting for transfers between devices  82.5 us (62%)
  starting transfers between devices  33.4 us (25%)
  local copies, waits for them, and re-layouts  14.3 us (11%)
  matrix products  1.52 us (1%)
  between operations  1.44 us (1%)
    all_to_all x1, waiting for transfers between devices, shards(): lax.all_to_all(ordered.reshape(seq_count * tp_count, 2, feature_count), (...  42.6 us
    all_to_all x1, waiting for transfers between devices, shards(): lax.all_to_all(by_position, 'seq', split_axis=0, concat_axis=0, tiled=True)  39.8 us
    all_to_all x1, starting transfers between devices, shards(): lax.all_to_all(by_position, 'seq', split_axis=0, concat_axis=0, tiled=True)  19.3 us
    all_to_all x1, starting transfers between devices, shards(): lax.all_to_all(ordered.reshape(seq_count * tp_count, 2, feature_count), (...  14.1 us
    unnamed x15, local copies, waits for them, and re-layouts  2.94 us
  transfers between devices with their start and end apart: 2, of which 2 were waited for; matrix products, arithmetic and copies ran while one was open for 3% of the time, Pallas kernels for 0%

profile of v2, /device:TPU:1, one launch (start us, length us, event | category | flops | bytes accessed | tf_op | source)
XLA Modules:
  0.0 134.2 jit_solution(14978547987810108337)
XLA Ops:
  0.0 2.9 %copy.51 = bf16[2,1,64,3072]{3,0,2,1:T(2,128)(2,1)} copy(bf16[2,1,64,3072]{3,2,1,0:T(8,128)(2,1)} %param.5) | data formatting | bytes 1572864 | tf_op args[0]
  2.9 19.3 %all-to-all-start = ((bf16[64,2,3072]{2,1,0:T(2,128)(2,1)}), bf16[64,2,3072]{2,1,0:T(2,128)(2,1)S(1)}, u32[]{:S(2)}, u32[]{:S(2)}) async-start(bf16[64,2,3072]{2,1,0:T(2,128)(2,1)} %bitcast.65), calls=%async_computation | async-start | bytes 1572864 | tf_op jit(solution)/shard_map/all_to_all | solution.py:67
  22.2 0.1 select_reduce_fusion
  22.3 0.8 gather_fusion
  23.1 39.8 %all-to-all-done = bf16[64,2,3072]{2,1,0:T(2,128)(2,1)S(1)} async-done(((bf16[64,2,3072]{2,1,0:T(2,128)(2,1)}), bf16[64,2,3072]{2,1,0:T(2,128)(2,1)S(1)}, u32[]{:S(2)}, u32[]{:S(2)}) %all-to-all-start) | async-done | bytes 786464 | tf_op jit(solution)/shard_map/all_to_all | solution.py:67
  63.0 2.1 %gather_fusion.1 = bf16[64,2,3072]{2,1,0:T(2,128)(2,1)S(1)} fusion(bf16[64,2,3072]{2,1,0:T(2,128)(2,1)S(1)} %all-to-all-done, s32[1024]{0:T(1024)S(1)} %pad_clamp_fusion), kind=kCustom, calls=%fused_computation.1 | custom fusion | bytes 1573120 | tf_op jit(solution)/shard_map/jit(_take)/gather | solution.py:68
  65.1 0.5 gather.21
  65.6 0.0 copy-start.6
  65.6 0.0 copy-start.2
  65.6 0.2 fusion.8
  65.8 1.7 %copy.36 = bf16[512,2,384]{2,1,0:T(2,128)(2,1)} copy(bf16[512,2,384]{2,0,1:T(8,128)(2,1)S(1)} %fusion.8) | data formatting | bytes 1572864 | tf_op jit(solution)/shard_map/reshape | solution.py:72
  67.5 14.1 %all-to-all-start.1 = ((bf16[512,2,384]{2,1,0:T(2,128)(2,1)}), bf16[512,2,384]{2,1,0:T(2,128)(2,1)S(1)}, u32[]{:S(2)}, u32[]{:S(2)}) async-start(bf16[512,2,384]{2,1,0:T(2,128)(2,1)} %copy.36), calls=%async_computation.1 | async-start | bytes 1572864 | tf_op jit(solution)/shard_map/all_to_all | solution.py:71
  81.6 0.6 dynamic-slice.4
  82.9 0.6 dynamic-slice.5
  83.5 0.1 fusion.26
  83.5 0.1 copy.38
  83.7 0.0 copy-start
  83.7 0.1 copy.39
  83.9 0.8 copy.42
  85.3 0.4 fusion.27
  85.7 0.2 convert_reduce_fusion.1
  85.8 42.6 %all-to-all-done.1 = bf16[512,2,384]{2,1,0:T(2,128)(2,1)S(1)} async-done(((bf16[512,2,384]{2,1,0:T(2,128)(2,1)}), bf16[512,2,384]{2,1,0:T(2,128)(2,1)S(1)}, u32[]{:S(2)}, u32[]{:S(2)}) %all-to-all-start.1) | async-done | bytes 786464 | tf_op jit(solution)/shard_map/all_to_all | solution.py:71
  128.5 1.1 fusion.25
  129.6 0.0 copy-start.1
  129.6 1.0 copy.40
  130.6 1.0 copy.37
  131.6 0.5 bitcast_reduce_fusion
  132.2 0.5 convert_reduce_fusion
  132.7 0.3 fusion.3
  133.0 0.0 copy-done.3
  133.1 0.3 fusion.7
  133.4 0.8 copy.44
  (16 shorter events, 0.1 us)
Async XLA Ops:
  0.0 22.1 %copy-start.4 = (s32[64]{0:T(128)S(1)}, s32[64]{0:T(128)}, u32[]{:S(2)}) copy-start(s32[64]{0:T(128)} %param.8) | copy-start | bytes 772
  0.0 22.2 %copy-start.5 = (s32[64]{0:T(128)S(1)}, s32[64]{0:T(128)}, u32[]{:S(2)}) copy-start(s32[64]{0:T(128)} %param.9) | copy-start | bytes 772
  2.9 60.1 %all-to-all-start = ((bf16[64,2,3072]{2,1,0:T(2,128)(2,1)}), bf16[64,2,3072]{2,1,0:T(2,128)(2,1)S(1)}, u32[]{:S(2)}, u32[]{:S(2)}) async-start(bf16[64,2,3072]{2,1,0:T(2,128)(2,1)} %bitcast.65), calls=%async_computation | async-start | bytes 1572864 | tf_op jit(solution)/shard_map/all_to_all | solution.py:67
  65.6 17.3 %copy-start.6 = (s32[64]{0:T(128)S(1)}, s32[64]{0:T(128)}, u32[]{:S(2)}) copy-start(s32[64]{0:T(128)} %param.6) | copy-start | bytes 772
  65.6 17.9 %copy-start.2 = (bf16[3,1,256,384]{3,2,1,0:T(8,128)(2,1)S(1)}, bf16[3,1,256,384]{3,2,1,0:T(8,128)(2,1)}, u32[]{:S(2)}) copy-start(bf16[3,1,256,384]{3,2,1,0:T(8,128)(2,1)} %param.7) | copy-start | bytes 1769476
  67.5 61.0 %all-to-all-start.1 = ((bf16[512,2,384]{2,1,0:T(2,128)(2,1)}), bf16[512,2,384]{2,1,0:T(2,128)(2,1)S(1)}, u32[]{:S(2)}, u32[]{:S(2)}) async-start(bf16[512,2,384]{2,1,0:T(2,128)(2,1)} %copy.36), calls=%async_computation.1 | async-start | bytes 1572864 | tf_op jit(solution)/shard_map/all_to_all | solution.py:71
  83.7 2.1 %copy-start = (bf16[1,1,256,384]{2,3,1,0:T(8,128)(2,1)}, bf16[1,1,256,384]{2,3,1,0:T(8,128)(2,1)S(1)}, u32[]{:S(2)}) copy-start(bf16[1,1,256,384]{2,3,1,0:T(8,128)(2,1)S(1)} %copy.38) | copy-start | bytes 589828
  129.6 2.0 %copy-start.1 = (bf16[1,1,256,384]{2,3,1,0:T(8,128)(2,1)S(1)}, bf16[1,1,256,384]{2,3,1,0:T(8,128)(2,1)}, u32[]{:S(2)}) copy-start(bf16[1,1,256,384]{2,3,1,0:T(8,128)(2,1)} %copy-done) | copy-start | bytes 589828
  132.1 0.9 copy-start.3

commit v3 on v2

--- a/solution.py
+++ b/solution.py
@@ -63,10 +63,10 @@
     seq_count = source_slot.shape[0]
     tp_count = cache.shape[3] // feature_count
     local_positions = cache.shape[2]
-    by_position = jnp.transpose(cache[:, 0], (1, 0, 2))
-    spread = lax.all_to_all(by_position, "seq", split_axis=0, concat_axis=0, tiled=True)
+    pair_rows = cache[:, 0].reshape(2 * local_positions, -1)
+    spread = lax.all_to_all(pair_rows, "seq", split_axis=0, concat_axis=0, tiled=True)
+    spread = spread.reshape(seq_count, 2, tp_count, feature_count)
     ordered = jnp.take(spread, source_slot, axis=0)
-    ordered = ordered.reshape(seq_count, 2, tp_count, feature_count)
     ordered = jnp.transpose(ordered, (0, 2, 1, 3))
     moved = lax.all_to_all(
         ordered.reshape(seq_count * tp_count, 2, feature_count),
@@ -75,11 +75,15 @@
         concat_axis=0,
         tiled=True,
     )
-    row_total = moved.shape[0]
-    old_keys = moved[:, 0].reshape(row_total, head_count, HD)
-    old_values = moved[:, 1].reshape(row_total, head_count, HD)
+    half = moved.shape[0] // 2
+    row_total = half * 2
+    old_keys = moved[:half].reshape(row_total, head_count, HD)
+    old_values = moved[half:].reshape(row_total, head_count, HD)
     rows = jnp.arange(row_total, dtype=jnp.int32)
-    positions = (rows % tp_count) * local_positions + rows // tp_count
+    pair = rows % 2
+    source_tp = (rows // 2) % tp_count
+    source_seq = rows // (2 * tp_count)
+    positions = source_tp * local_positions + 2 * source_seq + pair
     live = (positions < length)[None, :]
     cache_part = partial_part(queries, old_keys, old_values, live, factor)
     context = combine_parts(cache_part, group_part)

time: 134 us -> 132 us (0.985)
  local copies, waits for them, and re-layouts: 14.3 us -> 10.7 us
    unnamed x15 -> x8, local copies, waits for them, and re-layouts: 2.94 us -> 0.02 us
    all_to_all x0 -> x1, local copies, waits for them, and re-layouts: none -> 2.87 us  [shards(): lax.all_to_all(pair_rows, 'seq', split_axis=0, concat_axis=0, tiled=True)]
    slice x3 -> x1, local copies, waits for them, and re-layouts: 3.09 us -> 0.54 us  [shards(): old_values = moved[half:].reshape(row_total, head_count, HD)]
    gather x2 -> x1, local copies, waits for them, and re-layouts: 2.63 us -> 0.72 us  [shards(): ordered = jnp.take(spread, source_slot, axis=0)]
    reshape x0 -> x3, local copies, waits for them, and re-layouts: none -> 1.45 us  [the longest x1 0.5 us: shards(): spread = spread.reshape(seq_count, 2, tp_count, feature_count)]
where the time goes in v3:
time: 132 us; the launch traced here: 131 us
  waiting for transfers between devices  83 us (63%)
  starting transfers between devices  33.4 us (25%)
  local copies, waits for them, and re-layouts  10.7 us (8%)
  matrix products  1.86 us (1%)
  between operations  1.47 us (1%)
    all_to_all x1, waiting for transfers between devices, shards(): lax.all_to_all(ordered.reshape(seq_count * tp_count, 2, feature_count), (...  43.2 us
    all_to_all x1, waiting for transfers between devices, shards(): lax.all_to_all(pair_rows, 'seq', split_axis=0, concat_axis=0, tiled=True)  39.8 us
    all_to_all x1, starting transfers between devices, shards(): lax.all_to_all(pair_rows, 'seq', split_axis=0, concat_axis=0, tiled=True)  19.3 us
    all_to_all x1, starting transfers between devices, shards(): lax.all_to_all(ordered.reshape(seq_count * tp_count, 2, feature_count), (...  14.1 us
    all_to_all x1, local copies, waits for them, and re-layouts, shards(): lax.all_to_all(pair_rows, 'seq', split_axis=0, concat_axis=0, tiled=True)  2.87 us
  transfers between devices with their start and end apart: 2, of which 2 were waited for; matrix products, arithmetic and copies ran while one was open for 3% of the time, Pallas kernels for 0%

profile of v3, /device:TPU:1, one launch (start us, length us, event | category | flops | bytes accessed | tf_op | source)
XLA Modules:
  0.0 131.5 jit_solution(7545708497742830133)
XLA Ops:
  0.0 2.9 %all_to_all.9 = bf16[64,2,3072]{2,1,0:T(2,128)(2,1)} reshape(bf16[2,1,64,3072]{3,2,1,0:T(8,128)(2,1)} %param.5) | data formatting | bytes 1572864 | tf_op jit(solution)/shard_map/all_to_all | solution.py:67
  2.9 19.3 %all-to-all-start = ((bf16[64,2,3072]{2,1,0:T(2,128)(2,1)}), bf16[64,2,3072]{2,1,0:T(2,128)(2,1)S(1)}, u32[]{:S(2)}, u32[]{:S(2)}) async-start(bf16[64,2,3072]{2,1,0:T(2,128)(2,1)} %all_to_all.9), calls=%async_computation | async-start | bytes 1572864 | tf_op jit(solution)/shard_map/all_to_all | solution.py:67
  22.2 0.0 copy-done.1
  22.2 0.0 copy-done.2
  22.2 0.1 select_reduce_fusion
  22.3 0.8 gather_fusion
  23.1 39.8 %all-to-all-done = bf16[64,2,3072]{2,1,0:T(2,128)(2,1)S(1)} async-done(((bf16[64,2,3072]{2,1,0:T(2,128)(2,1)}), bf16[64,2,3072]{2,1,0:T(2,128)(2,1)S(1)}, u32[]{:S(2)}, u32[]{:S(2)}) %all-to-all-start) | async-done | bytes 786464 | tf_op jit(solution)/shard_map/all_to_all | solution.py:67
  63.0 0.5 reshape.127
  63.5 0.7 gather_fusion.1
  64.2 0.0 copy-start.3
  64.2 0.0 copy-start
  64.2 0.2 copy_bitcast_fusion
  64.4 1.7 %copy.42 = bf16[512,2,384]{2,1,0:T(2,128)(2,1)} copy(bf16[512,2,384]{2,0,1:T(8,128)(2,1)S(1)} %copy_bitcast_fusion) | data formatting | bytes 1572864 | tf_op jit(solution)/shard_map/reshape | solution.py:72
  66.1 14.1 %all-to-all-start.1 = ((bf16[512,2,384]{2,1,0:T(2,128)(2,1)}), bf16[512,2,384]{2,1,0:T(2,128)(2,1)S(1)}, u32[]{:S(2)}, u32[]{:S(2)}) async-start(bf16[512,2,384]{2,1,0:T(2,128)(2,1)} %copy.42), calls=%async_computation.1 | async-start | bytes 1572864 | tf_op jit(solution)/shard_map/all_to_all | solution.py:71
  80.2 0.7 dynamic-slice.4
  81.5 0.0 copy-done.3
  81.5 0.7 dynamic-slice.5
  82.2 0.1 fusion.32
  82.3 0.1 copy.43
  82.4 0.1 copy.45
  82.6 0.1 copy.48
  83.4 0.4 fusion.33
  83.8 0.2 convert_reduce_fusion.1
  83.9 43.2 %all-to-all-done.1 = bf16[512,2,384]{2,1,0:T(2,128)(2,1)S(1)} async-done(((bf16[512,2,384]{2,1,0:T(2,128)(2,1)}), bf16[512,2,384]{2,1,0:T(2,128)(2,1)S(1)}, u32[]{:S(2)}, u32[]{:S(2)}) %all-to-all-start.1) | async-done | bytes 786464 | tf_op jit(solution)/shard_map/all_to_all | solution.py:71
  127.1 0.5 fusion.31
  127.7 0.5 reshape.129
  128.2 0.5 reshape.130
  128.6 0.4 bitcast_reduce_fusion
  129.1 0.5 convert_reduce_fusion
  129.6 0.3 fusion.6
  129.9 0.7 fusion.7
  130.7 0.8 copy.50
  (10 shorter events, 0.1 us)
Async XLA Ops:
  0.0 22.2 %copy-start.1 = (s32[64]{0:T(128)S(1)}, s32[64]{0:T(128)}, u32[]{:S(2)}) copy-start(s32[64]{0:T(128)} %param.8) | copy-start | bytes 772
  0.0 22.2 %copy-start.2 = (s32[64]{0:T(128)S(1)}, s32[64]{0:T(128)}, u32[]{:S(2)}) copy-start(s32[64]{0:T(128)} %param.9) | copy-start | bytes 772
  2.9 60.1 %all-to-all-start = ((bf16[64,2,3072]{2,1,0:T(2,128)(2,1)}), bf16[64,2,3072]{2,1,0:T(2,128)(2,1)S(1)}, u32[]{:S(2)}, u32[]{:S(2)}) async-start(bf16[64,2,3072]{2,1,0:T(2,128)(2,1)} %all_to_all.9), calls=%async_computation | async-start | bytes 1572864 | tf_op jit(solution)/shard_map/all_to_all | solution.py:67
  64.2 17.3 %copy-start.3 = (s32[64]{0:T(128)S(1)}, s32[64]{0:T(128)}, u32[]{:S(2)}) copy-start(s32[64]{0:T(128)} %param.6) | copy-start | bytes 772
  64.2 18.0 %copy-start = (bf16[3,1,256,384]{3,2,1,0:T(8,128)(2,1)S(1)}, bf16[3,1,256,384]{3,2,1,0:T(8,128)(2,1)}, u32[]{:S(2)}) copy-start(bf16[3,1,256,384]{3,2,1,0:T(8,128)(2,1)} %param.7) | copy-start | bytes 1769476
  66.1 61.0 %all-to-all-start.1 = ((bf16[512,2,384]{2,1,0:T(2,128)(2,1)}), bf16[512,2,384]{2,1,0:T(2,128)(2,1)S(1)}, u32[]{:S(2)}, u32[]{:S(2)}) async-start(bf16[512,2,384]{2,1,0:T(2,128)(2,1)} %copy.42), calls=%async_computation.1 | async-start | bytes 1572864 | tf_op jit(solution)/shard_map/all_to_all | solution.py:71

commit v4 on v3

--- a/solution.py
+++ b/solution.py
@@ -63,11 +63,10 @@
     seq_count = source_slot.shape[0]
     tp_count = cache.shape[3] // feature_count
     local_positions = cache.shape[2]
-    pair_rows = cache[:, 0].reshape(2 * local_positions, -1)
+    pair_rows = cache[:, 0].reshape(seq_count, 2, tp_count, feature_count)
+    pair_rows = jnp.transpose(pair_rows, (0, 2, 1, 3))
     spread = lax.all_to_all(pair_rows, "seq", split_axis=0, concat_axis=0, tiled=True)
-    spread = spread.reshape(seq_count, 2, tp_count, feature_count)
     ordered = jnp.take(spread, source_slot, axis=0)
-    ordered = jnp.transpose(ordered, (0, 2, 1, 3))
     moved = lax.all_to_all(
         ordered.reshape(seq_count * tp_count, 2, feature_count),
         ("seq", "tp"),

time: 132 us -> 132 us (level)
  other arithmetic: 1.06 us -> 3.49 us
  local copies, waits for them, and re-layouts: 10.7 us -> 8.61 us
    all_to_all x1 -> x0, local copies, waits for them, and re-layouts: 2.87 us -> none  [shards(): lax.all_to_all(pair_rows, 'seq', split_axis=0, concat_axis=0, tiled=True)]
    select_n x0 -> x1, other arithmetic: none -> 2.64 us  [shards(): ordered = jnp.take(spread, source_slot, axis=0)]
    reshape x2 -> x0, local copies, waits for them, and re-layouts: 2.18 us -> none  [the longest x1 1.69 us: shards(): ordered.reshape(seq_count * tp_count, 2, feature_count)]
    unnamed x8 -> x9, local copies, waits for them, and re-layouts: 0.02 us -> 2.19 us
where the time goes in v4:
time: 132 us
  waiting for transfers between devices  82.9 us (63%)
  starting transfers between devices  33.4 us (25%)
  local copies, waits for them, and re-layouts  8.61 us (7%)
  other arithmetic  3.49 us (3%)
  matrix products  1.85 us (1%)
  between operations  1.47 us (1%)
    all_to_all x1, waiting for transfers between devices, shards(): lax.all_to_all(ordered.reshape(seq_count * tp_count, 2, feature_count), (...  43.2 us
    all_to_all x1, waiting for transfers between devices, shards(): lax.all_to_all(pair_rows, 'seq', split_axis=0, concat_axis=0, tiled=True)  39.7 us
    all_to_all x1, starting transfers between devices, shards(): lax.all_to_all(pair_rows, 'seq', split_axis=0, concat_axis=0, tiled=True)  19.3 us
    all_to_all x1, starting transfers between devices, shards(): lax.all_to_all(ordered.reshape(seq_count * tp_count, 2, feature_count), (...  14.1 us
  transfers between devices with their start and end apart: 2, of which 2 were waited for; matrix products, arithmetic and copies ran while one was open for 3% of the time, Pallas kernels for 0%

profile of v4, /device:TPU:1, one launch (start us, length us, event | category | flops | bytes accessed | tf_op | source)
XLA Modules:
  0.0 131.7 jit_solution(9858900098897541946)
XLA Ops:
  0.0 2.2 %copy.33 = bf16[16,8,8,384]{3,2,1,0:T(8,128)(2,1)} copy(bf16[16,8,8,384]{3,1,2,0:T(8,128)(2,1)} %bitcast.64) | data formatting | bytes 1572864
  2.2 19.3 %all-to-all-start = ((bf16[64,8,2,384]{3,1,2,0:T(8,128)(2,1)}), bf16[64,8,2,384]{3,1,2,0:T(8,128)(2,1)S(1)}, u32[]{:S(2)}, u32[]{:S(2)}) async-start(bf16[64,8,2,384]{3,1,2,0:T(8,128)(2,1)} %bitcast.4), calls=%async_computation | async-start | bytes 1572864 | tf_op jit(solution)/shard_map/all_to_all | solution.py:68
  21.5 0.0 copy-done.1
  21.5 0.0 copy-done.2
  21.5 0.1 select_reduce_fusion
  21.6 0.8 gather_fusion
  22.4 0.1 broadcast_in_dim.84
  22.5 0.1 broadcast_in_dim.85
  22.6 39.7 %all-to-all-done = bf16[64,8,2,384]{3,1,2,0:T(8,128)(2,1)S(1)} async-done(((bf16[64,8,2,384]{3,1,2,0:T(8,128)(2,1)}), bf16[64,8,2,384]{3,1,2,0:T(8,128)(2,1)S(1)}, u32[]{:S(2)}, u32[]{:S(2)}) %all-to-all-start) | async-done | bytes 786464 | tf_op jit(solution)/shard_map/all_to_all | solution.py:68
  62.3 0.7 gather_fusion.1
  63.0 0.0 copy-start.3
  63.0 0.0 copy-start
  63.0 0.6 copy.22
  63.6 2.6 %broadcast_select_fusion = bf16[512,2,384]{2,1,0:T(2,128)(2,1)} fusion(pred[512]{0:T(512)(128)(4,1)S(1)} %broadcast_in_dim.85, bf16[64,8,2,384]{3,2,1,0:T(2,128)(2,1)S(1)} %copy.22), kind=kLoop, calls=%fused_computation.8 | loop fusion | flops 393216 | bytes 1573376 | tf_op jit(solution)/shard_map/jit(_take)/select_n | solution.py:69
  66.3 14.1 %all-to-all-start.1 = ((bf16[512,2,384]{2,1,0:T(2,128)(2,1)}), bf16[512,2,384]{2,1,0:T(2,128)(2,1)S(1)}, u32[]{:S(2)}, u32[]{:S(2)}) async-start(bf16[512,2,384]{2,1,0:T(2,128)(2,1)} %broadcast_select_fusion), calls=%async_computation.1 | async-start | bytes 1572864 | tf_op jit(solution)/shard_map/all_to_all | solution.py:70
  80.4 0.7 dynamic-slice.4
  81.7 0.7 dynamic-slice.5
  82.4 0.1 fusion.32
  82.4 0.1 copy.23
  82.6 0.1 copy.25
  82.7 0.1 copy.28
  83.6 0.4 fusion.33
  83.9 0.2 convert_reduce_fusion.1
  84.1 43.2 %all-to-all-done.1 = bf16[512,2,384]{2,1,0:T(2,128)(2,1)S(1)} async-done(((bf16[512,2,384]{2,1,0:T(2,128)(2,1)}), bf16[512,2,384]{2,1,0:T(2,128)(2,1)S(1)}, u32[]{:S(2)}, u32[]{:S(2)}) %all-to-all-start.1) | async-done | bytes 786464 | tf_op jit(solution)/shard_map/all_to_all | solution.py:70
  127.3 0.5 fusion.31
  127.8 0.5 reshape.120
  128.3 0.5 reshape.121
  128.8 0.4 bitcast_reduce_fusion
  129.3 0.5 convert_reduce_fusion
  129.8 0.3 fusion.6
  130.1 0.7 fusion.7
  130.8 0.8 copy.30
  (11 shorter events, 0.1 us)
Async XLA Ops:
  0.0 21.5 %copy-start.1 = (s32[64]{0:T(128)S(1)}, s32[64]{0:T(128)}, u32[]{:S(2)}) copy-start(s32[64]{0:T(128)} %param.8) | copy-start | bytes 772
  0.0 21.5 %copy-start.2 = (s32[64]{0:T(128)S(1)}, s32[64]{0:T(128)}, u32[]{:S(2)}) copy-start(s32[64]{0:T(128)} %param.9) | copy-start | bytes 772
  2.2 60.1 %all-to-all-start = ((bf16[64,8,2,384]{3,1,2,0:T(8,128)(2,1)}), bf16[64,8,2,384]{3,1,2,0:T(8,128)(2,1)S(1)}, u32[]{:S(2)}, u32[]{:S(2)}) async-start(bf16[64,8,2,384]{3,1,2,0:T(8,128)(2,1)} %bitcast.4), calls=%async_computation | async-start | bytes 1572864 | tf_op jit(solution)/shard_map/all_to_all | solution.py:68
  63.0 18.7 %copy-start.3 = (s32[64]{0:T(128)S(1)}, s32[64]{0:T(128)}, u32[]{:S(2)}) copy-start(s32[64]{0:T(128)} %param.6) | copy-start | bytes 772
  63.0 19.4 %copy-start = (bf16[3,1,256,384]{3,2,1,0:T(8,128)(2,1)S(1)}, bf16[3,1,256,384]{3,2,1,0:T(8,128)(2,1)}, u32[]{:S(2)}) copy-start(bf16[3,1,256,384]{3,2,1,0:T(8,128)(2,1)} %param.7) | copy-start | bytes 1769476
  66.3 61.0 %all-to-all-start.1 = ((bf16[512,2,384]{2,1,0:T(2,128)(2,1)}), bf16[512,2,384]{2,1,0:T(2,128)(2,1)S(1)}, u32[]{:S(2)}, u32[]{:S(2)}) async-start(bf16[512,2,384]{2,1,0:T(2,128)(2,1)} %broadcast_select_fusion), calls=%async_computation.1 | async-start | bytes 1572864 | tf_op jit(solution)/shard_map/all_to_all | solution.py:70

commit v5 on v4

--- a/solution.py
+++ b/solution.py
@@ -66,7 +66,7 @@
     pair_rows = cache[:, 0].reshape(seq_count, 2, tp_count, feature_count)
     pair_rows = jnp.transpose(pair_rows, (0, 2, 1, 3))
     spread = lax.all_to_all(pair_rows, "seq", split_axis=0, concat_axis=0, tiled=True)
-    ordered = jnp.take(spread, source_slot, axis=0)
+    ordered = jnp.take(spread, source_slot, axis=0, mode="clip")
     moved = lax.all_to_all(
         ordered.reshape(seq_count * tp_count, 2, feature_count),
         ("seq", "tp"),

time: 132 us -> 130 us (0.985)
  other arithmetic: 3.49 us -> 0.85 us
    select_n x1 -> x0, other arithmetic: 2.64 us -> none  [shards(): ordered = jnp.take(spread, source_slot, axis=0)]
where the time goes in v5:
time: 130 us
  waiting for transfers between devices  83 us (64%)
  starting transfers between devices  33.4 us (26%)
  local copies, waits for them, and re-layouts  9.31 us (7%)
  matrix products  1.86 us (1%)
  between operations  1.45 us (1%)
    all_to_all x1, waiting for transfers between devices, shards(): lax.all_to_all(ordered.reshape(seq_count * tp_count, 2, feature_count), (...  43.2 us
    all_to_all x1, waiting for transfers between devices, shards(): lax.all_to_all(pair_rows, 'seq', split_axis=0, concat_axis=0, tiled=True)  39.8 us
    all_to_all x1, starting transfers between devices, shards(): lax.all_to_all(pair_rows, 'seq', split_axis=0, concat_axis=0, tiled=True)  19.3 us
    all_to_all x1, starting transfers between devices, shards(): lax.all_to_all(ordered.reshape(seq_count * tp_count, 2, feature_count), (...  14.1 us
  transfers between devices with their start and end apart: 2, of which 2 were waited for; matrix products, arithmetic and copies ran while one was open for 3% of the time, Pallas kernels for 0%

profile of v5, /device:TPU:1, one launch (start us, length us, event | category | flops | bytes accessed | tf_op | source)
XLA Modules:
  0.0 129.9 jit_solution(4540050573429922557)
XLA Ops:
  0.0 0.0 copy-start.2
  0.0 2.2 %copy.33 = bf16[16,8,8,384]{3,2,1,0:T(8,128)(2,1)} copy(bf16[16,8,8,384]{3,1,2,0:T(8,128)(2,1)} %bitcast.63) | data formatting | bytes 1572864
  2.2 19.3 %all-to-all-start = ((bf16[64,8,2,384]{3,1,2,0:T(8,128)(2,1)}), bf16[64,8,2,384]{3,1,2,0:T(8,128)(2,1)S(1)}, u32[]{:S(2)}, u32[]{:S(2)}) async-start(bf16[64,8,2,384]{3,1,2,0:T(8,128)(2,1)} %bitcast.4), calls=%async_computation | async-start | bytes 1572864 | tf_op jit(solution)/shard_map/all_to_all | solution.py:68
  21.5 0.0 copy-done.2
  21.5 0.0 copy-done.1
  21.5 0.1 select_reduce_fusion
  21.6 0.8 gather_fusion
  22.4 0.0 copy-start.3
  22.4 0.0 copy-start
  22.4 39.8 %all-to-all-done = bf16[64,8,2,384]{3,1,2,0:T(8,128)(2,1)S(1)} async-done(((bf16[64,8,2,384]{3,1,2,0:T(8,128)(2,1)}), bf16[64,8,2,384]{3,1,2,0:T(8,128)(2,1)S(1)}, u32[]{:S(2)}, u32[]{:S(2)}) %all-to-all-start) | async-done | bytes 786464 | tf_op jit(solution)/shard_map/all_to_all | solution.py:68
  62.3 0.7 gather_fusion.1
  63.0 1.5 %copy.22 = bf16[64,8,2,384]{3,2,1,0:T(2,128)(2,1)} copy(bf16[64,8,2,384]{3,1,2,0:T(8,128)(2,1)S(1)} %gather_fusion.1) | data formatting | bytes 1572864 | tf_op jit(solution)/shard_map/jit(_take)/gather | solution.py:69
  64.5 14.1 %all-to-all-start.1 = ((bf16[512,2,384]{2,1,0:T(2,128)(2,1)}), bf16[512,2,384]{2,1,0:T(2,128)(2,1)S(1)}, u32[]{:S(2)}, u32[]{:S(2)}) async-start(bf16[512,2,384]{2,1,0:T(2,128)(2,1)} %bitcast.5), calls=%async_computation.1 | async-start | bytes 1572864 | tf_op jit(solution)/shard_map/all_to_all | solution.py:70
  78.6 0.7 dynamic-slice.4
  79.9 0.0 copy-done.3
  79.9 0.7 dynamic-slice.5
  80.6 0.0 copy-done
  80.6 0.1 fusion.32
  80.6 0.1 copy.23
  80.8 0.1 copy.25
  80.9 0.1 copy.28
  81.8 0.4 fusion.33
  82.2 0.2 convert_reduce_fusion.1
  82.3 43.2 %all-to-all-done.1 = bf16[512,2,384]{2,1,0:T(2,128)(2,1)S(1)} async-done(((bf16[512,2,384]{2,1,0:T(2,128)(2,1)}), bf16[512,2,384]{2,1,0:T(2,128)(2,1)S(1)}, u32[]{:S(2)}, u32[]{:S(2)}) %all-to-all-start.1) | async-done | bytes 786464 | tf_op jit(solution)/shard_map/all_to_all | solution.py:70
  125.5 0.5 fusion.31
  126.1 0.5 reshape.113
  126.5 0.5 reshape.114
  127.0 0.4 bitcast_reduce_fusion
  127.5 0.5 convert_reduce_fusion
  128.0 0.3 fusion.6
  128.3 0.7 fusion.7
  129.0 0.8 copy.30
  (8 shorter events, 0.1 us)
Async XLA Ops:
  0.0 21.5 %copy-start.2 = (s32[64]{0:T(128)S(1)}, s32[64]{0:T(128)}, u32[]{:S(2)}) copy-start(s32[64]{0:T(128)} %param.8) | copy-start | bytes 772
  0.0 21.5 %copy-start.1 = (s32[64]{0:T(128)S(1)}, s32[64]{0:T(128)}, u32[]{:S(2)}) copy-start(s32[64]{0:T(128)} %param.9) | copy-start | bytes 772
  2.2 60.1 %all-to-all-start = ((bf16[64,8,2,384]{3,1,2,0:T(8,128)(2,1)}), bf16[64,8,2,384]{3,1,2,0:T(8,128)(2,1)S(1)}, u32[]{:S(2)}, u32[]{:S(2)}) async-start(bf16[64,8,2,384]{3,1,2,0:T(8,128)(2,1)} %bitcast.4), calls=%async_computation | async-start | bytes 1572864 | tf_op jit(solution)/shard_map/all_to_all | solution.py:68
  22.4 57.5 %copy-start.3 = (s32[64]{0:T(128)S(1)}, s32[64]{0:T(128)}, u32[]{:S(2)}) copy-start(s32[64]{0:T(128)} %param.6) | copy-start | bytes 772
  22.4 58.2 %copy-start = (bf16[3,1,256,384]{3,2,1,0:T(8,128)(2,1)S(1)}, bf16[3,1,256,384]{3,2,1,0:T(8,128)(2,1)}, u32[]{:S(2)}) copy-start(bf16[3,1,256,384]{3,2,1,0:T(8,128)(2,1)} %param.7) | copy-start | bytes 1769476
  64.5 61.0 %all-to-all-start.1 = ((bf16[512,2,384]{2,1,0:T(2,128)(2,1)}), bf16[512,2,384]{2,1,0:T(2,128)(2,1)S(1)}, u32[]{:S(2)}, u32[]{:S(2)}) async-start(bf16[512,2,384]{2,1,0:T(2,128)(2,1)} %bitcast.5), calls=%async_computation.1 | async-start | bytes 1572864 | tf_op jit(solution)/shard_map/all_to_all | solution.py:70

commit v6 on v5

--- a/solution.py
+++ b/solution.py
@@ -66,22 +66,24 @@
     pair_rows = cache[:, 0].reshape(seq_count, 2, tp_count, feature_count)
     pair_rows = jnp.transpose(pair_rows, (0, 2, 1, 3))
     spread = lax.all_to_all(pair_rows, "seq", split_axis=0, concat_axis=0, tiled=True)
-    ordered = jnp.take(spread, source_slot, axis=0, mode="clip")
+    spread = jnp.transpose(spread, (1, 0, 2, 3))
+    ordered = jnp.take(spread, source_slot, axis=1, mode="clip")
     moved = lax.all_to_all(
         ordered.reshape(seq_count * tp_count, 2, feature_count),
-        ("seq", "tp"),
+        ("tp", "seq"),
         split_axis=0,
         concat_axis=0,
         tiled=True,
     )
-    half = moved.shape[0] // 2
-    row_total = half * 2
-    old_keys = moved[:half].reshape(row_total, head_count, HD)
-    old_values = moved[half:].reshape(row_total, head_count, HD)
+    moved = moved.reshape(tp_count, seq_count, 2, feature_count)
+    half = seq_count // 2
+    row_total = tp_count * half * 2
+    old_keys = moved[:, :half].reshape(row_total, head_count, HD)
+    old_values = moved[:, half:].reshape(row_total, head_count, HD)
     rows = jnp.arange(row_total, dtype=jnp.int32)
     pair = rows % 2
-    source_tp = (rows // 2) % tp_count
-    source_seq = rows // (2 * tp_count)
+    source_seq = (rows // 2) % half
+    source_tp = rows // (2 * half)
     positions = source_tp * local_positions + 2 * source_seq + pair
     live = (positions < length)[None, :]
     cache_part = partial_part(queries, old_keys, old_values, live, factor)

time: 130 us -> 128 us (0.985)
  waiting for transfers between devices: 83 us -> 80.8 us
    all_to_all x1, waiting for transfers between devices: 43.2 us -> 41 us  [shards(): lax.all_to_all(ordered.reshape(seq_count * tp_count, 2, feature_count), (...]
    reshape x2 -> x3, local copies, waits for them, and re-layouts: 0.95 us -> 2.64 us  [the longest x1 1.69 us: shards(): ordered.reshape(seq_count * tp_count, 2, feature_count)]
    gather x2, local copies, waits for them, and re-layouts: 2.23 us -> 0.9 us  [shards(): ordered = jnp.take(spread, source_slot, axis=1, mode='clip')]
where the time goes in v6:
time: 128 us
  waiting for transfers between devices  80.8 us (63%)
  starting transfers between devices  33.4 us (26%)
  local copies, waits for them, and re-layouts  9.71 us (8%)
  matrix products  1.86 us (1%)
  between operations  1.46 us (1%)
    all_to_all x1, waiting for transfers between devices, shards(): lax.all_to_all(ordered.reshape(seq_count * tp_count, 2, feature_count), (...  41 us
    all_to_all x1, waiting for transfers between devices, shards(): lax.all_to_all(pair_rows, 'seq', split_axis=0, concat_axis=0, tiled=True)  39.9 us
    all_to_all x1, starting transfers between devices, shards(): lax.all_to_all(pair_rows, 'seq', split_axis=0, concat_axis=0, tiled=True)  19.3 us
    all_to_all x1, starting transfers between devices, shards(): lax.all_to_all(ordered.reshape(seq_count * tp_count, 2, feature_count), (...  14.1 us
  transfers between devices with their start and end apart: 2, of which 2 were waited for; matrix products, arithmetic and copies ran while one was open for 3% of the time, Pallas kernels for 0%

profile of v6, /device:TPU:1, one launch (start us, length us, event | category | flops | bytes accessed | tf_op | source)
XLA Modules:
  0.0 128.1 jit_solution(2025679213714485559)
XLA Ops:
  0.0 2.2 %copy.55 = bf16[16,8,8,384]{3,2,1,0:T(8,128)(2,1)} copy(bf16[16,8,8,384]{3,1,2,0:T(8,128)(2,1)} %bitcast.70) | data formatting | bytes 1572864
  2.2 19.3 %all-to-all-start = ((bf16[64,8,2,384]{3,1,2,0:T(8,128)(2,1)}), bf16[64,8,2,384]{3,1,2,0:T(8,128)(2,1)S(1)}, u32[]{:S(2)}, u32[]{:S(2)}) async-start(bf16[64,8,2,384]{3,1,2,0:T(8,128)(2,1)} %bitcast.4), calls=%async_computation | async-start | bytes 1572864 | tf_op jit(solution)/shard_map/all_to_all | solution.py:68
  21.5 0.0 copy-done.2
  21.5 0.0 copy-done.1
  21.5 0.1 select_reduce_fusion
  21.6 0.8 gather_fusion
  22.4 39.9 %all-to-all-done = bf16[64,8,2,384]{3,1,2,0:T(8,128)(2,1)S(1)} async-done(((bf16[64,8,2,384]{3,1,2,0:T(8,128)(2,1)}), bf16[64,8,2,384]{3,1,2,0:T(8,128)(2,1)S(1)}, u32[]{:S(2)}, u32[]{:S(2)}) %all-to-all-start) | async-done | bytes 786464 | tf_op jit(solution)/shard_map/all_to_all | solution.py:68
  62.3 0.7 gather_fusion.1
  63.0 0.0 copy-start.3
  63.0 0.0 copy-start
  63.0 0.2 copy.43
  63.2 1.7 %copy.44 = bf16[512,2,384]{2,1,0:T(2,128)(2,1)} copy(bf16[512,2,384]{2,0,1:T(8,128)(2,1)S(1)} %bitcast.68) | data formatting | bytes 1572864 | tf_op jit(solution)/shard_map/reshape | solution.py:72
  64.9 14.1 %all-to-all-start.1 = ((bf16[512,2,384]{2,1,0:T(2,128)(2,1)}), bf16[512,2,384]{2,1,0:T(2,128)(2,1)S(1)}, u32[]{:S(2)}, u32[]{:S(2)}) async-start(bf16[512,2,384]{2,1,0:T(2,128)(2,1)} %copy.44), calls=%async_computation.1 | async-start | bytes 1572864 | tf_op jit(solution)/shard_map/all_to_all | solution.py:71
  79.0 0.7 dynamic-slice.4
  80.3 0.0 copy-done.3
  80.3 0.7 dynamic-slice.5
  81.0 0.0 copy-done
  81.0 0.1 fusion.32
  81.0 0.1 copy.45
  81.2 0.1 copy.47
  81.3 0.1 copy.50
  82.2 0.4 fusion.33
  82.5 0.2 convert_reduce_fusion.1
  82.7 41.0 %all-to-all-done.1 = bf16[512,2,384]{2,1,0:T(2,128)(2,1)S(1)} async-done(((bf16[512,2,384]{2,1,0:T(2,128)(2,1)}), bf16[512,2,384]{2,1,0:T(2,128)(2,1)S(1)}, u32[]{:S(2)}, u32[]{:S(2)}) %all-to-all-start.1) | async-done | bytes 786464 | tf_op jit(solution)/shard_map/all_to_all | solution.py:71
  123.7 0.6 fusion.31
  124.3 0.5 reshape.117
  124.7 0.5 reshape.118
  125.2 0.4 bitcast_reduce_fusion
  125.7 0.5 convert_reduce_fusion
  126.2 0.3 fusion.6
  126.5 0.7 fusion.7
  127.3 0.8 copy.52
  (9 shorter events, 0.1 us)
Async XLA Ops:
  0.0 21.5 %copy-start.2 = (s32[64]{0:T(128)S(1)}, s32[64]{0:T(128)}, u32[]{:S(2)}) copy-start(s32[64]{0:T(128)} %param.8) | copy-start | bytes 772
  0.0 21.5 %copy-start.1 = (s32[64]{0:T(128)S(1)}, s32[64]{0:T(128)}, u32[]{:S(2)}) copy-start(s32[64]{0:T(128)} %param.9) | copy-start | bytes 772
  2.2 60.1 %all-to-all-start = ((bf16[64,8,2,384]{3,1,2,0:T(8,128)(2,1)}), bf16[64,8,2,384]{3,1,2,0:T(8,128)(2,1)S(1)}, u32[]{:S(2)}, u32[]{:S(2)}) async-start(bf16[64,8,2,384]{3,1,2,0:T(8,128)(2,1)} %bitcast.4), calls=%async_computation | async-start | bytes 1572864 | tf_op jit(solution)/shard_map/all_to_all | solution.py:68
  63.0 17.3 %copy-start.3 = (s32[64]{0:T(128)S(1)}, s32[64]{0:T(128)}, u32[]{:S(2)}) copy-start(s32[64]{0:T(128)} %param.6) | copy-start | bytes 772
  63.0 18.0 %copy-start = (bf16[3,1,256,384]{3,2,1,0:T(8,128)(2,1)S(1)}, bf16[3,1,256,384]{3,2,1,0:T(8,128)(2,1)}, u32[]{:S(2)}) copy-start(bf16[3,1,256,384]{3,2,1,0:T(8,128)(2,1)} %param.7) | copy-start | bytes 1769476
  64.9 58.8 %all-to-all-start.1 = ((bf16[512,2,384]{2,1,0:T(2,128)(2,1)}), bf16[512,2,384]{2,1,0:T(2,128)(2,1)S(1)}, u32[]{:S(2)}, u32[]{:S(2)}) async-start(bf16[512,2,384]{2,1,0:T(2,128)(2,1)} %copy.44), calls=%async_computation.1 | async-start | bytes 1572864 | tf_op jit(solution)/shard_map/all_to_all | solution.py:71

commit v7 on v6

--- a/solution.py
+++ b/solution.py
@@ -1,8 +1,11 @@
 import math
+
+import functools
 
 import jax
 import jax.numpy as jnp
 from jax import lax
+from jax.sharding import Mesh
 from jax.sharding import PartitionSpec as P
 
 HD = 96
@@ -42,11 +45,11 @@
     return result.reshape(result.shape[0], -1).astype(jnp.bfloat16)
 
 
-def shards(cache, cache_len, group, group_req, req_order):
+def shards(inner, cache, cache_len, group, group_req, req_order):
     factor = 1.0 / math.sqrt(HD)
     slot_of = inverse_table(req_order)
     source_slot = jnp.take(slot_of, group_req)
-    my_request = jnp.take(group_req, lax.axis_index("seq"))
+    my_request = jnp.take(group_req, lax.axis_index(("outer", "inner")))
     length = jnp.take(cache_len, my_request)
     row_count = group.shape[2]
     feature_count = group.shape[3]
@@ -65,12 +68,19 @@
     local_positions = cache.shape[2]
     pair_rows = cache[:, 0].reshape(seq_count, 2, tp_count, feature_count)
     pair_rows = jnp.transpose(pair_rows, (0, 2, 1, 3))
-    spread = lax.all_to_all(pair_rows, "seq", split_axis=0, concat_axis=0, tiled=True)
+    spread = lax.all_to_all(
+        pair_rows, ("inner", "outer"), split_axis=0, concat_axis=0, tiled=True
+    )
+    outer = seq_count // inner
+    numbers = jnp.arange(seq_count, dtype=jnp.int32)
+    needing = (numbers % outer) * inner + numbers // outer
+    wanted = jnp.take(source_slot, needing, mode="clip")
+    place = (wanted % inner) * outer + wanted // inner
     spread = jnp.transpose(spread, (1, 0, 2, 3))
-    ordered = jnp.take(spread, source_slot, axis=1, mode="clip")
+    ordered = jnp.take(spread, place, axis=1, mode="clip")
     moved = lax.all_to_all(
         ordered.reshape(seq_count * tp_count, 2, feature_count),
-        ("tp", "seq"),
+        ("tp", "inner", "outer"),
         split_axis=0,
         concat_axis=0,
         tiled=True,
@@ -92,6 +102,24 @@
 
 
 def solution(mesh):
-    in_specs = (P(None, "seq", "tp", None), P(), P(None, "seq", None, "tp"), P(), P())
-    out_specs = P("seq", None, "tp")
-    return jax.shard_map(shards, mesh=mesh, in_specs=in_specs, out_specs=out_specs, check_vma=False)
+    seq_devices = mesh.devices[:, 0]
+    try:
+        inner = len({device.coords[1] for device in seq_devices})
+    except AttributeError:
+        inner = 1
+    if inner < 1 or seq_devices.shape[0] % inner:
+        inner = 1
+    outer = seq_devices.shape[0] // inner
+    split_mesh = Mesh(
+        mesh.devices.reshape(outer, inner, mesh.devices.shape[1]), ("outer", "inner", "tp")
+    )
+    seq = ("outer", "inner")
+    in_specs = (P(None, seq, "tp", None), P(), P(None, seq, None, "tp"), P(), P())
+    out_specs = P(seq, None, "tp")
+    return jax.shard_map(
+        functools.partial(shards, inner),
+        mesh=split_mesh,
+        in_specs=in_specs,
+        out_specs=out_specs,
+        check_vma=False,
+    )

time: 128 us -> 129 us (level)
    all_to_all x1, waiting for transfers between devices: 39.9 us -> 38.2 us  [shards(): lax.all_to_all(pair_rows, ('inner', 'outer'), split_axis=0, concat_axis=0...]
    all_to_all x1, waiting for transfers between devices: 41 us -> 42.3 us  [shards(): lax.all_to_all(ordered.reshape(seq_count * tp_count, 2, feature_count), (...]
where the time goes in v7:
time: 129 us
  waiting for transfers between devices  80.5 us (62%)
  starting transfers between devices  33.8 us (26%)
  local copies, waits for them, and re-layouts  10.5 us (8%)
  matrix products  1.86 us (1%)
  between operations  1.48 us (1%)
    all_to_all x1, waiting for transfers between devices, shards(): lax.all_to_all(ordered.reshape(seq_count * tp_count, 2, feature_count), (...  42.3 us
    all_to_all x1, waiting for transfers between devices, shards(): lax.all_to_all(pair_rows, ('inner', 'outer'), split_axis=0, concat_axis=0...  38.2 us
    all_to_all x1, starting transfers between devices, shards(): lax.all_to_all(pair_rows, ('inner', 'outer'), split_axis=0, concat_axis=0...  19.3 us
    all_to_all x1, starting transfers between devices, shards(): lax.all_to_all(ordered.reshape(seq_count * tp_count, 2, feature_count), (...  14.5 us
  transfers between devices with their start and end apart: 2, of which 2 were waited for; matrix products, arithmetic and copies ran while one was open for 3% of the time, Pallas kernels for 0%

profile of v7, /device:TPU:1, one launch (start us, length us, event | category | flops | bytes accessed | tf_op | source)
XLA Modules:
  0.0 129.0 jit_solution(7328272507444573853)
XLA Ops:
  0.0 2.2 %copy.55 = bf16[16,8,8,384]{3,2,1,0:T(8,128)(2,1)} copy(bf16[16,8,8,384]{3,1,2,0:T(8,128)(2,1)} %bitcast.89) | data formatting | bytes 1572864
  2.2 19.3 %all-to-all-start = ((bf16[64,8,2,384]{3,1,2,0:T(8,128)(2,1)}), bf16[64,8,2,384]{3,1,2,0:T(8,128)(2,1)S(1)}, u32[]{:S(2)}, u32[]{:S(2)}) async-start(bf16[64,8,2,384]{3,1,2,0:T(8,128)(2,1)} %bitcast.4), calls=%async_computation | async-start | bytes 1572864 | tf_op jit(solution)/shard_map/all_to_all | solution.py:71
  21.5 0.0 copy-done.2
  21.5 0.0 copy-done.1
  21.5 0.1 select_reduce_fusion
  21.6 0.8 gather_fusion
  22.4 0.8 gather_fusion.1
  23.2 38.2 %all-to-all-done = bf16[64,8,2,384]{3,1,2,0:T(8,128)(2,1)S(1)} async-done(((bf16[64,8,2,384]{3,1,2,0:T(8,128)(2,1)}), bf16[64,8,2,384]{3,1,2,0:T(8,128)(2,1)S(1)}, u32[]{:S(2)}, u32[]{:S(2)}) %all-to-all-start) | async-done | bytes 786464 | tf_op jit(solution)/shard_map/all_to_all | solution.py:71
  61.4 0.7 gather_fusion.2
  62.1 0.0 copy-start.3
  62.1 0.0 copy-start
  62.1 0.2 copy.43
  62.3 1.7 %copy.44 = bf16[512,2,384]{2,1,0:T(2,128)(2,1)} copy(bf16[512,2,384]{2,0,1:T(8,128)(2,1)S(1)} %bitcast.87) | data formatting | bytes 1572864 | tf_op jit(solution)/shard_map/reshape | solution.py:82
  64.0 14.5 %all-to-all-start.1 = ((bf16[512,2,384]{2,1,0:T(2,128)(2,1)}), bf16[512,2,384]{2,1,0:T(2,128)(2,1)S(1)}, u32[]{:S(2)}, u32[]{:S(2)}) async-start(bf16[512,2,384]{2,1,0:T(2,128)(2,1)} %copy.44), calls=%async_computation.1 | async-start | bytes 1572864 | tf_op jit(solution)/shard_map/all_to_all | solution.py:81
  78.5 0.7 dynamic-slice.4
  79.8 0.0 copy-done.3
  79.8 0.7 dynamic-slice.5
  80.5 0.1 fusion.38
  80.5 0.1 copy.45
  80.7 0.1 copy.47
  80.8 0.1 copy.50
  81.7 0.4 fusion.39
  82.0 0.2 convert_reduce_fusion.1
  82.2 42.3 %all-to-all-done.1 = bf16[512,2,384]{2,1,0:T(2,128)(2,1)S(1)} async-done(((bf16[512,2,384]{2,1,0:T(2,128)(2,1)}), bf16[512,2,384]{2,1,0:T(2,128)(2,1)S(1)}, u32[]{:S(2)}, u32[]{:S(2)}) %all-to-all-start.1) | async-done | bytes 786464 | tf_op jit(solution)/shard_map/all_to_all | solution.py:81
  124.6 0.6 fusion.37
  125.1 0.5 reshape.245
  125.6 0.5 reshape.246
  126.1 0.4 bitcast_reduce_fusion
  126.6 0.5 convert_reduce_fusion
  127.1 0.3 fusion.6
  127.4 0.7 fusion.7
  128.1 0.8 copy.52
  (13 shorter events, 0.1 us)
Async XLA Ops:
  0.0 21.5 %copy-start.2 = (s32[64]{0:T(128)S(1)}, s32[64]{0:T(128)}, u32[]{:S(2)}) copy-start(s32[64]{0:T(128)} %param.8) | copy-start | bytes 772
  0.0 21.5 %copy-start.1 = (s32[64]{0:T(128)S(1)}, s32[64]{0:T(128)}, u32[]{:S(2)}) copy-start(s32[64]{0:T(128)} %param.9) | copy-start | bytes 772
  2.2 59.2 %all-to-all-start = ((bf16[64,8,2,384]{3,1,2,0:T(8,128)(2,1)}), bf16[64,8,2,384]{3,1,2,0:T(8,128)(2,1)S(1)}, u32[]{:S(2)}, u32[]{:S(2)}) async-start(bf16[64,8,2,384]{3,1,2,0:T(8,128)(2,1)} %bitcast.4), calls=%async_computation | async-start | bytes 1572864 | tf_op jit(solution)/shard_map/all_to_all | solution.py:71
  62.1 17.7 %copy-start.3 = (s32[64]{0:T(128)S(1)}, s32[64]{0:T(128)}, u32[]{:S(2)}) copy-start(s32[64]{0:T(128)} %param.6) | copy-start | bytes 772
  62.1 18.3 %copy-start = (bf16[3,1,256,384]{3,2,1,0:T(8,128)(2,1)S(1)}, bf16[3,1,256,384]{3,2,1,0:T(8,128)(2,1)}, u32[]{:S(2)}) copy-start(bf16[3,1,256,384]{3,2,1,0:T(8,128)(2,1)} %param.7) | copy-start | bytes 1769476
  64.0 60.5 %all-to-all-start.1 = ((bf16[512,2,384]{2,1,0:T(2,128)(2,1)}), bf16[512,2,384]{2,1,0:T(2,128)(2,1)S(1)}, u32[]{:S(2)}, u32[]{:S(2)}) async-start(bf16[512,2,384]{2,1,0:T(2,128)(2,1)} %copy.44), calls=%async_computation.1 | async-start | bytes 1572864 | tf_op jit(solution)/shard_map/all_to_all | solution.py:81

commit v8 on v7

--- a/solution.py
+++ b/solution.py
@@ -72,29 +72,26 @@
         pair_rows, ("inner", "outer"), split_axis=0, concat_axis=0, tiled=True
     )
     outer = seq_count // inner
-    numbers = jnp.arange(seq_count, dtype=jnp.int32)
-    needing = (numbers % outer) * inner + numbers // outer
-    wanted = jnp.take(source_slot, needing, mode="clip")
-    place = (wanted % inner) * outer + wanted // inner
+    place = (source_slot % inner) * outer + source_slot // inner
     spread = jnp.transpose(spread, (1, 0, 2, 3))
     ordered = jnp.take(spread, place, axis=1, mode="clip")
     moved = lax.all_to_all(
         ordered.reshape(seq_count * tp_count, 2, feature_count),
-        ("tp", "inner", "outer"),
+        ("tp", "outer", "inner"),
         split_axis=0,
         concat_axis=0,
         tiled=True,
     )
-    moved = moved.reshape(tp_count, seq_count, 2, feature_count)
-    half = seq_count // 2
-    row_total = tp_count * half * 2
-    old_keys = moved[:, :half].reshape(row_total, head_count, HD)
-    old_values = moved[:, half:].reshape(row_total, head_count, HD)
+    moved = moved.reshape(tp_count, outer, 2, inner // 2, 2, feature_count)
+    row_total = seq_count * tp_count
+    old_keys = moved[:, :, 0].reshape(row_total, head_count, HD)
+    old_values = moved[:, :, 1].reshape(row_total, head_count, HD)
     rows = jnp.arange(row_total, dtype=jnp.int32)
     pair = rows % 2
-    source_seq = (rows // 2) % half
-    source_tp = rows // (2 * half)
-    positions = source_tp * local_positions + 2 * source_seq + pair
+    low_y = (rows // 2) % (inner // 2)
+    source_z = (rows // inner) % outer
+    source_tp = rows // (inner * outer)
+    positions = source_tp * local_positions + 2 * (low_y * outer + source_z) + pair
     live = (positions < length)[None, :]
     cache_part = partial_part(queries, old_keys, old_values, live, factor)
     context = combine_parts(cache_part, group_part)

time: 129 us -> 128 us (level)
    all_to_all x1, waiting for transfers between devices: 42.3 us -> 41 us  [shards(): lax.all_to_all(ordered.reshape(seq_count * tp_count, 2, feature_count), (...]
where the time goes in v8:
time: 128 us
  waiting for transfers between devices  79.9 us (62%)
  starting transfers between devices  33.8 us (26%)
  local copies, waits for them, and re-layouts  9.85 us (8%)
  matrix products  1.85 us (1%)
  between operations  1.48 us (1%)
    all_to_all x1, waiting for transfers between devices, shards(): lax.all_to_all(ordered.reshape(seq_count * tp_count, 2, feature_count), (...  41 us
    all_to_all x1, waiting for transfers between devices, shards(): lax.all_to_all(pair_rows, ('inner', 'outer'), split_axis=0, concat_axis=0...  39 us
    all_to_all x1, starting transfers between devices, shards(): lax.all_to_all(pair_rows, ('inner', 'outer'), split_axis=0, concat_axis=0...  19.3 us
    all_to_all x1, starting transfers between devices, shards(): lax.all_to_all(ordered.reshape(seq_count * tp_count, 2, feature_count), (...  14.5 us
  transfers between devices with their start and end apart: 2, of which 2 were waited for; matrix products, arithmetic and copies ran while one was open for 3% of the time, Pallas kernels for 0%

profile of v8, /device:TPU:1, one launch (start us, length us, event | category | flops | bytes accessed | tf_op | source)
XLA Modules:
  0.0 127.7 jit_solution(2749638636507698757)
XLA Ops:
  0.0 2.2 %copy.53 = bf16[16,8,8,384]{3,2,1,0:T(8,128)(2,1)} copy(bf16[16,8,8,384]{3,1,2,0:T(8,128)(2,1)} %bitcast.70) | data formatting | bytes 1572864
  2.2 19.3 %all-to-all-start = ((bf16[64,8,2,384]{3,1,2,0:T(8,128)(2,1)}), bf16[64,8,2,384]{3,1,2,0:T(8,128)(2,1)S(1)}, u32[]{:S(2)}, u32[]{:S(2)}) async-start(bf16[64,8,2,384]{3,1,2,0:T(8,128)(2,1)} %bitcast.4), calls=%async_computation | async-start | bytes 1572864 | tf_op jit(solution)/shard_map/all_to_all | solution.py:71
  21.5 0.0 copy-done.2
  21.5 0.0 copy-done.1
  21.5 0.1 select_reduce_fusion
  21.6 0.8 gather_fusion
  22.4 39.0 %all-to-all-done = bf16[64,8,2,384]{3,1,2,0:T(8,128)(2,1)S(1)} async-done(((bf16[64,8,2,384]{3,1,2,0:T(8,128)(2,1)}), bf16[64,8,2,384]{3,1,2,0:T(8,128)(2,1)S(1)}, u32[]{:S(2)}, u32[]{:S(2)}) %all-to-all-start) | async-done | bytes 786464 | tf_op jit(solution)/shard_map/all_to_all | solution.py:71
  61.4 0.7 gather_fusion.1
  62.1 0.0 copy-start.3
  62.1 0.0 copy-start
  62.1 0.2 copy.41
  62.3 1.7 %copy.42 = bf16[512,2,384]{2,1,0:T(2,128)(2,1)} copy(bf16[512,2,384]{2,0,1:T(8,128)(2,1)S(1)} %bitcast.68) | data formatting | bytes 1572864 | tf_op jit(solution)/shard_map/reshape | solution.py:79
  64.0 14.5 %all-to-all-start.1 = ((bf16[512,2,384]{2,1,0:T(2,128)(2,1)}), bf16[512,2,384]{2,1,0:T(2,128)(2,1)S(1)}, u32[]{:S(2)}, u32[]{:S(2)}) async-start(bf16[512,2,384]{2,1,0:T(2,128)(2,1)} %copy.42), calls=%async_computation.1 | async-start | bytes 1572864 | tf_op jit(solution)/shard_map/all_to_all | solution.py:78
  78.5 0.7 dynamic-slice.4
  79.8 0.0 copy-done.3
  79.8 0.7 dynamic-slice.5
  80.5 0.0 copy-done
  80.5 0.1 fusion.39
  80.5 0.1 copy.43
  80.7 0.1 copy.45
  80.8 0.1 copy.48
  81.7 0.4 fusion.40
  82.0 0.2 convert_reduce_fusion.1
  82.2 41.0 %all-to-all-done.1 = bf16[512,2,384]{2,1,0:T(2,128)(2,1)S(1)} async-done(((bf16[512,2,384]{2,1,0:T(2,128)(2,1)}), bf16[512,2,384]{2,1,0:T(2,128)(2,1)S(1)}, u32[]{:S(2)}, u32[]{:S(2)}) %all-to-all-start.1) | async-done | bytes 786464 | tf_op jit(solution)/shard_map/all_to_all | solution.py:78
  123.2 0.7 fusion.38
  123.9 0.5 reshape_squeeze.19
  124.4 0.5 reshape_squeeze.22
  124.9 0.4 bitcast_reduce_fusion
  125.3 0.5 convert_reduce_fusion
  125.8 0.3 fusion.6
  126.2 0.7 fusion.7
  126.9 0.8 copy.50
  (9 shorter events, 0.1 us)
Async XLA Ops:
  0.0 21.5 %copy-start.2 = (s32[64]{0:T(128)S(1)}, s32[64]{0:T(128)}, u32[]{:S(2)}) copy-start(s32[64]{0:T(128)} %param.8) | copy-start | bytes 772
  0.0 21.5 %copy-start.1 = (s32[64]{0:T(128)S(1)}, s32[64]{0:T(128)}, u32[]{:S(2)}) copy-start(s32[64]{0:T(128)} %param.9) | copy-start | bytes 772
  2.2 59.2 %all-to-all-start = ((bf16[64,8,2,384]{3,1,2,0:T(8,128)(2,1)}), bf16[64,8,2,384]{3,1,2,0:T(8,128)(2,1)S(1)}, u32[]{:S(2)}, u32[]{:S(2)}) async-start(bf16[64,8,2,384]{3,1,2,0:T(8,128)(2,1)} %bitcast.4), calls=%async_computation | async-start | bytes 1572864 | tf_op jit(solution)/shard_map/all_to_all | solution.py:71
  62.1 17.7 %copy-start.3 = (s32[64]{0:T(128)S(1)}, s32[64]{0:T(128)}, u32[]{:S(2)}) copy-start(s32[64]{0:T(128)} %param.6) | copy-start | bytes 772
  62.1 18.3 %copy-start = (bf16[3,1,256,384]{3,2,1,0:T(8,128)(2,1)S(1)}, bf16[3,1,256,384]{3,2,1,0:T(8,128)(2,1)}, u32[]{:S(2)}) copy-start(bf16[3,1,256,384]{3,2,1,0:T(8,128)(2,1)} %param.7) | copy-start | bytes 1769476
  64.0 59.2 %all-to-all-start.1 = ((bf16[512,2,384]{2,1,0:T(2,128)(2,1)}), bf16[512,2,384]{2,1,0:T(2,128)(2,1)S(1)}, u32[]{:S(2)}, u32[]{:S(2)}) async-start(bf16[512,2,384]{2,1,0:T(2,128)(2,1)} %copy.42), calls=%async_computation.1 | async-start | bytes 1572864 | tf_op jit(solution)/shard_map/all_to_all | solution.py:78

commit v9 on v6

--- a/solution.py
+++ b/solution.py
@@ -78,15 +78,35 @@
     moved = moved.reshape(tp_count, seq_count, 2, feature_count)
     half = seq_count // 2
     row_total = tp_count * half * 2
-    old_keys = moved[:, :half].reshape(row_total, head_count, HD)
-    old_values = moved[:, half:].reshape(row_total, head_count, HD)
+    old_keys = moved[:, :half].reshape(row_total, feature_count)
+    old_values = moved[:, half:].reshape(row_total, feature_count)
     rows = jnp.arange(row_total, dtype=jnp.int32)
     pair = rows % 2
     source_seq = (rows // 2) % half
     source_tp = rows // (2 * half)
     positions = source_tp * local_positions + 2 * source_seq + pair
     live = (positions < length)[None, :]
-    cache_part = partial_part(queries, old_keys, old_values, live, factor)
+    flat_queries = group[0, 0]
+    tops, sums, mixes = [], [], []
+    for head in range(head_count):
+        columns = slice(head * HD, (head + 1) * HD)
+        head_scores = (
+            jnp.dot(
+                flat_queries[:, columns],
+                old_keys[:, columns].T,
+                preferred_element_type=jnp.float32,
+            )
+            * factor
+        )
+        head_scores = jnp.where(live, head_scores, -jnp.inf)
+        head_top = jnp.max(head_scores, axis=-1)
+        head_weights = jnp.exp(head_scores - head_top[:, None]).astype(jnp.bfloat16)
+        sums.append(jnp.sum(head_weights, axis=-1, dtype=jnp.float32))
+        mixes.append(
+            jnp.dot(head_weights, old_values[:, columns], preferred_element_type=jnp.float32)
+        )
+        tops.append(head_top)
+    cache_part = (jnp.stack(tops), jnp.stack(sums), jnp.stack(mixes))
     context = combine_parts(cache_part, group_part)
     return context[None]
 

time: 128 us -> 130 us (1.016)
  local copies, waits for them, and re-layouts: 9.71 us -> 11.7 us
  waiting for transfers between devices: 80.8 us -> 79.1 us
    dot_general x0 -> x8, matrix products: none -> 2.43 us  [the longest x4 1.32 us: shards(): jnp.dot(flat_queries[:, columns], old_keys[:, columns].T, preferred_eleme...]
    unnamed x9 -> x11, local copies, waits for them, and re-layouts: 2.19 us -> 4.21 us
where the time goes in v9:
time: 130 us
  waiting for transfers between devices  79.1 us (61%)
  starting transfers between devices  33.5 us (26%)
  local copies, waits for them, and re-layouts  11.7 us (9%)
  matrix products  3.11 us (2%)
  between operations  1.4 us (1%)
    all_to_all x1, waiting for transfers between devices, shards(): lax.all_to_all(ordered.reshape(seq_count * tp_count, 2, feature_count), (...  39.8 us
    all_to_all x1, waiting for transfers between devices, shards(): lax.all_to_all(pair_rows, 'seq', split_axis=0, concat_axis=0, tiled=True)  39.2 us
    all_to_all x1, starting transfers between devices, shards(): lax.all_to_all(pair_rows, 'seq', split_axis=0, concat_axis=0, tiled=True)  19.4 us
    all_to_all x1, starting transfers between devices, shards(): lax.all_to_all(ordered.reshape(seq_count * tp_count, 2, feature_count), (...  14.1 us
    unnamed x11, local copies, waits for them, and re-layouts  4.21 us
  transfers between devices with their start and end apart: 2, of which 2 were waited for; matrix products, arithmetic and copies ran while one was open for 3% of the time, Pallas kernels for 0%

profile of v9, /device:TPU:1, one launch (start us, length us, event | category | flops | bytes accessed | tf_op | source)
XLA Modules:
  0.0 129.6 jit_solution(6529186631940316541)
XLA Ops:
  0.0 2.1 %copy.39 = bf16[16,8,8,384]{3,2,1,0:T(8,128)(2,1)} copy(bf16[16,8,8,384]{3,1,2,0:T(8,128)(2,1)} %bitcast.46) | data formatting | bytes 1572864
  2.1 19.4 %all-to-all-start = ((bf16[64,8,2,384]{3,1,2,0:T(8,128)(2,1)}), bf16[64,8,2,384]{3,1,2,0:T(8,128)(2,1)S(1)}, u32[]{:S(2)}, u32[]{:S(2)}) async-start(bf16[64,8,2,384]{3,1,2,0:T(8,128)(2,1)} %bitcast.4), calls=%async_computation | async-start | bytes 1572864 | tf_op jit(solution)/shard_map/all_to_all | solution.py:68
  21.6 0.6 copy-done.2
  22.3 0.8 gather_fusion
  23.1 39.2 %all-to-all-done = bf16[64,8,2,384]{3,1,2,0:T(8,128)(2,1)S(1)} async-done(((bf16[64,8,2,384]{3,1,2,0:T(8,128)(2,1)}), bf16[64,8,2,384]{3,1,2,0:T(8,128)(2,1)S(1)}, u32[]{:S(2)}, u32[]{:S(2)}) %all-to-all-start) | async-done | bytes 786464 | tf_op jit(solution)/shard_map/all_to_all | solution.py:68
  62.4 0.7 gather_fusion.1
  63.1 0.2 copy.31
  63.3 1.7 %copy.32 = bf16[512,2,384]{2,1,0:T(2,128)(2,1)} copy(bf16[512,2,384]{2,0,1:T(8,128)(2,1)S(1)} %bitcast.45) | data formatting | bytes 1572864 | tf_op jit(solution)/shard_map/reshape | solution.py:72
  65.0 14.1 %all-to-all-start.1 = ((bf16[512,2,384]{2,1,0:T(2,128)(2,1)}), bf16[512,2,384]{2,1,0:T(2,128)(2,1)S(1)}, u32[]{:S(2)}, u32[]{:S(2)}) async-start(bf16[512,2,384]{2,1,0:T(2,128)(2,1)} %copy.32), calls=%async_computation.1 | async-start | bytes 1572864 | tf_op jit(solution)/shard_map/all_to_all | solution.py:71
  79.1 0.7 dynamic-slice.4
  80.4 0.6 copy-done.4
  81.0 0.6 dynamic-slice.5
  81.7 0.1 copy.34
  81.8 0.1 copy.33
  82.0 0.8 copy.35
  83.4 0.4 fusion.45
  83.8 0.2 convert_reduce_fusion
  83.9 39.8 %all-to-all-done.1 = bf16[512,2,384]{2,1,0:T(2,128)(2,1)S(1)} async-done(((bf16[512,2,384]{2,1,0:T(2,128)(2,1)}), bf16[512,2,384]{2,1,0:T(2,128)(2,1)S(1)}, u32[]{:S(2)}, u32[]{:S(2)}) %all-to-all-start.1) | async-done | bytes 786464 | tf_op jit(solution)/shard_map/all_to_all | solution.py:71
  123.8 0.6 fusion.39
  124.3 0.1 reshape.264
  124.5 0.3 fusion.41
  124.8 0.3 fusion.42
  125.2 0.1 reshape.265
  125.5 0.3 convolution_bitcast_fusion
  125.9 0.3 convolution_bitcast_fusion.1
  126.2 0.3 fusion.43
  126.6 0.3 fusion.44
  127.0 0.3 convolution_bitcast_fusion.2
  127.3 0.2 convolution_bitcast_fusion.3
  127.7 0.8 copy-done.1
  128.4 0.3 fusion.7
  128.8 0.8 copy.37
  (20 shorter events, 0.8 us)
Async XLA Ops:
  2.1 19.4 %copy-start.3 = (s32[64]{0:T(128)S(1)}, s32[64]{0:T(128)}, u32[]{:S(2)}) copy-start(s32[64]{0:T(128)} %param.8) | copy-start | bytes 772
  2.1 60.2 %all-to-all-start = ((bf16[64,8,2,384]{3,1,2,0:T(8,128)(2,1)}), bf16[64,8,2,384]{3,1,2,0:T(8,128)(2,1)S(1)}, u32[]{:S(2)}, u32[]{:S(2)}) async-start(bf16[64,8,2,384]{3,1,2,0:T(8,128)(2,1)} %bitcast.4), calls=%async_computation | async-start | bytes 1572864 | tf_op jit(solution)/shard_map/all_to_all | solution.py:68
  21.6 0.7 copy-start.2
  65.0 16.6 %copy-start = (bf16[3,1,256,384]{3,2,1,0:T(8,128)(2,1)S(1)}, bf16[3,1,256,384]{3,2,1,0:T(8,128)(2,1)}, u32[]{:S(2)}) copy-start(bf16[3,1,256,384]{3,2,1,0:T(8,128)(2,1)} %param.7) | copy-start | bytes 1769476
  65.0 58.8 %all-to-all-start.1 = ((bf16[512,2,384]{2,1,0:T(2,128)(2,1)}), bf16[512,2,384]{2,1,0:T(2,128)(2,1)S(1)}, u32[]{:S(2)}, u32[]{:S(2)}) async-start(bf16[512,2,384]{2,1,0:T(2,128)(2,1)} %copy.32), calls=%async_computation.1 | async-start | bytes 1572864 | tf_op jit(solution)/shard_map/all_to_all | solution.py:71
  80.4 0.7 copy-start.4
  127.5 0.9 copy-start.1
